TPU v7x, 512 devices: a whole 4x8x8 slice. The times are simulated.
512 devices in a mesh: section: 8 (over z), dp: 64 (over x, y, core).
Axes of the slice: x: 4, y: 8, z: 8, core: 2. Of those that a mesh axis runs over, the one named last changes fastest.
Arguments:
- images: bfloat16 [128, 12, 12, 256], P('dp'), may hold values from -6 to 6
- dw_kernel: bfloat16 [8, 49, 256], P('section'), may hold values from -0.875 to 0.875
- ln_gain: bfloat16 [8, 256], P('section'), may hold values from 0.5 to 1.5
- w_in: bfloat16 [8, 256, 1024], P('section'), may hold values from -0.375 to 0.375
- w_out: bfloat16 [8, 1024, 256], P('section'), may hold values from -0.1875 to 0.1875
- layer_scale: bfloat16 [8, 256], P('section'), may hold values from 0.19921875 to 1
- scene_grad: bfloat16 [384, 12, 12, 256], P('dp'), may hold values from -6 to 6
- view_slot: int32 [128], P('dp'), may hold values from 0 to 383, as said below
Outputs:
- grad_kernel: bfloat16 [8, 49, 256], P('section')
- grad_gain: bfloat16 [8, 256], P('section')
- grad_in: bfloat16 [8, 256, 1024], P('section', None, 'dp')
- grad_out: bfloat16 [8, 1024, 256], P('section', 'dp')
- grad_scale: bfloat16 [8, 256], P('section')
Inputs may be any that keep to these rules, and one draw needn't show every extreme that they name: `view_slot`: views v and w differ in slot unless v = w. Slot s is held by index s // 6 of dp; a view held by index d of dp has a slot held by d - 1, d or d + 1, and on holder o it is one of the slots (d - o + 1) * 2 to (d - o + 2) * 2 - 1 of that holder.
All inputs are finite; a program needn't handle non-finite values.
Results may differ from a plain program's by a relative error of at most 0.024.
Values may be sent and summed in bfloat16 or wider, within the bound.
No kernel may reach another device: no remote copies, remote signals or barrier semaphores. Data moves between devices by JAX's collectives and lax.ppermute only.
A program may use at most 64 MiB of HBM per device.

v0:
```python
import math

import jax
import jax.numpy as jnp
from jax import lax
from jax.sharding import PartitionSpec as P

ln_eps = 1e-06


def padded_2(block, sides, width):
    for axis, dim in sides:
        count = lax.axis_size(axis)
        forward = [(i, i + 1) for i in range(count - 1)]
        backward = [(target, source) for source, target in forward]
        low = lax.ppermute(
            lax.slice_in_dim(block, block.shape[dim] - width, None, axis=dim), axis, forward
        )
        high = lax.ppermute(lax.slice_in_dim(block, 0, width, axis=dim), axis, backward)
        block = jnp.concatenate([low, block, high], axis=dim)
    return block


def from_behind(block, axis, distance):
    devices = range(lax.axis_size(axis))
    route = [(i - distance, i) for i in devices if i - distance in devices]
    return lax.ppermute(block, axis, route)


def depthwise(inputs, kernel, ksize):
    height = inputs.shape[1]
    width = inputs.shape[2]
    margin = ksize // 2
    padded = jnp.pad(inputs, ((0, 0), (margin, margin), (margin, margin), (0, 0)))
    total = jnp.zeros(inputs.shape, jnp.float32)
    for row_tap in range(ksize):
        for col_tap in range(ksize):
            total = (
                total
                + padded[:, row_tap : row_tap + height, col_tap : col_tap + width, :]
                * kernel[row_tap * ksize + col_tap]
            )
    return total


def block_forward(inputs, params, ksize):
    kernel, norm_gain, proj_in, proj_out, scale = params
    channels = inputs.shape[-1]
    lead = inputs.shape[:-1]
    depthwise_output = depthwise(inputs.astype(jnp.float32), kernel, ksize)
    centered_input = jnp.mean(depthwise_output, axis=-1, keepdims=True)
    spread = jnp.mean((depthwise_output - centered_input) ** 2, axis=-1, keepdims=True)
    inverse_deviation = lax.rsqrt(spread + ln_eps)
    standardized_input = (depthwise_output - centered_input) * inverse_deviation
    normalized_input = (standardized_input * norm_gain).astype(jnp.bfloat16)
    channel_mixed = jnp.dot(
        normalized_input.reshape(-1, channels), proj_in, preferred_element_type=jnp.float32
    )
    hidden_expanded = jax.nn.gelu(channel_mixed, approximate=False).astype(jnp.bfloat16)
    residual_return = jnp.dot(
        hidden_expanded, proj_out, preferred_element_type=jnp.float32
    ).reshape(lead + (channels,))
    block_output = (inputs.astype(jnp.float32) + scale * residual_return).astype(jnp.bfloat16)
    return (
        block_output,
        (
            standardized_input,
            inverse_deviation,
            normalized_input,
            channel_mixed,
            hidden_expanded,
            residual_return,
        ),
    )


def block_backward(inputs, params, arrived, ksize):
    kernel, norm_gain, proj_in, proj_out, scale = params
    _, saved_residuals = block_forward(inputs, params, ksize)
    (
        standardized_input,
        inverse_deviation,
        normalized_input,
        channel_mixed,
        hidden_expanded,
        residual_return,
    ) = saved_residuals
    channels = inputs.shape[-1]
    height = inputs.shape[1]
    width = inputs.shape[2]
    lead = inputs.shape[:-1]
    incoming = arrived.astype(jnp.float32)
    g_scale = jnp.sum(incoming * residual_return, axis=(0, 1, 2))
    ct_back = (incoming * scale).astype(jnp.bfloat16).reshape(-1, channels)
    g_out = jnp.dot(hidden_expanded.T, ct_back, preferred_element_type=jnp.float32)
    ct_hidden = (
        jnp.dot(ct_back, proj_out.T, preferred_element_type=jnp.float32)
        .astype(jnp.bfloat16)
        .astype(jnp.float32)
    )
    slope = 0.5 * (1.0 + lax.erf(channel_mixed * (1.0 / math.sqrt(2.0)))) + channel_mixed * jnp.exp(
        -0.5 * channel_mixed * channel_mixed
    ) * (1.0 / math.sqrt(2.0 * math.pi))
    ct_mixed = (ct_hidden * slope).astype(jnp.bfloat16)
    g_in = jnp.dot(
        normalized_input.reshape(-1, channels).T, ct_mixed, preferred_element_type=jnp.float32
    )
    normalized_cotangent = (
        jnp.dot(ct_mixed, proj_in.T, preferred_element_type=jnp.float32)
        .astype(jnp.bfloat16)
        .astype(jnp.float32)
    )
    normalized_cotangent = normalized_cotangent.reshape(lead + (channels,))
    norm_gain_gradient = jnp.sum(normalized_cotangent * standardized_input, axis=(0, 1, 2))
    standardized_cotangent = normalized_cotangent * norm_gain
    depthwise_cotangent = inverse_deviation * (
        standardized_cotangent
        - jnp.mean(standardized_cotangent, axis=-1, keepdims=True)
        - standardized_input
        * jnp.mean(standardized_cotangent * standardized_input, axis=-1, keepdims=True)
    )
    margin = ksize // 2
    pad_spec = ((0, 0), (margin, margin), (margin, margin), (0, 0))
    padded_x = jnp.pad(inputs.astype(jnp.float32), pad_spec)
    padded_ct = jnp.pad(depthwise_cotangent, pad_spec)
    kernel_rows = []
    ct_inputs = incoming
    for row_tap in range(ksize):
        for col_tap in range(ksize):
            window = padded_x[:, row_tap : row_tap + height, col_tap : col_tap + width, :]
            kernel_rows.append(jnp.sum(depthwise_cotangent * window, axis=(0, 1, 2)))
            flip_row = ksize - 1 - row_tap
            flip_col = ksize - 1 - col_tap
            ct_inputs = (
                ct_inputs
                + padded_ct[:, flip_row : flip_row + height, flip_col : flip_col + width, :]
                * kernel[row_tap * ksize + col_tap]
            )
    g_kernel = jnp.stack(kernel_rows, axis=0)
    return (ct_inputs.astype(jnp.bfloat16), (g_kernel, norm_gain_gradient, g_in, g_out, g_scale))


def per_device(images, dw_kernel, ln_gain, w_in, w_out, layer_scale, scene_grad, view_slot):
    section_id = lax.axis_index("section")
    sections = lax.axis_size("section")
    holder_id = lax.axis_index("dp")
    holders = lax.axis_size("dp")
    views = images.shape[0]
    slot_dev = scene_grad.shape[0]
    ksize = math.isqrt(dw_kernel.shape[1])
    params = (
        dw_kernel[0].astype(jnp.float32),
        ln_gain[0].astype(jnp.float32),
        w_in[0],
        w_out[0],
        layer_scale[0].astype(jnp.float32),
    )
    holder = view_slot // slot_dev
    local_row = view_slot % slot_dev
    side = holder - holder_id + 1
    extended = padded_2(scene_grad, (("dp", 0),), slot_dev)
    rows = side * slot_dev + local_row
    targets = jnp.take(extended, rows, axis=0)
    ticks = views + sections - 1
    empty_map = jnp.zeros(images.shape[1:], jnp.bfloat16)

    def run_block(current):
        return block_forward(current[None], params, ksize)[0][0]

    def forward_tick(tick, carry):
        incoming, saved_residuals = carry
        micro = tick - section_id
        valid = (micro >= 0) & (micro < views)
        index = jnp.clip(micro, 0, views - 1)
        own_image = lax.dynamic_index_in_dim(
            images, jnp.clip(tick, 0, views - 1), 0, keepdims=False
        )
        current = jnp.where(section_id == 0, own_image, incoming)
        saved_residuals = jnp.where(
            valid,
            lax.dynamic_update_index_in_dim(saved_residuals, current, index, 0),
            saved_residuals,
        )
        result = run_block(current)
        incoming = from_behind(result, "section", 1)
        return (incoming, saved_residuals)

    _, saved_residuals = lax.fori_loop(0, ticks, forward_tick, (empty_map, jnp.zeros_like(images)))

    def backward_step(current, arrived):
        back_x, back_p = block_backward(current[None], params, arrived[None], ksize)
        return (back_x[0], back_p)

    start_totals = jax.tree.map(lambda member: jnp.zeros(member.shape, jnp.float32), params)

    def backward_tick(tick, carry):
        incoming, totals = carry
        micro = tick - (sections - 1 - section_id)
        valid = (micro >= 0) & (micro < views)
        index = jnp.clip(micro, 0, views - 1)
        own_target = lax.dynamic_index_in_dim(targets, index, 0, keepdims=False)
        arrived = jnp.where(section_id == sections - 1, own_target, incoming)
        current = lax.dynamic_index_in_dim(saved_residuals, index, 0, keepdims=False)
        back_x, back_p = backward_step(current, arrived)
        totals = jax.tree.map(
            lambda total, term: total + jnp.where(valid, term, 0.0), totals, back_p
        )
        incoming = from_behind(back_x, "section", -1)
        return (incoming, totals)

    _, totals = lax.fori_loop(0, ticks, backward_tick, (empty_map, start_totals))
    g_kernel, norm_gain_gradient, g_in, g_out, g_scale = totals
    share = g_in.shape[1] // holders
    s_kernel, s_gain, s_in, s_out, s_scale = lax.psum(
        (g_kernel, norm_gain_gradient, g_in, g_out, g_scale), "dp"
    )
    s_in = lax.dynamic_slice_in_dim(s_in, holder_id * share, share, 1)
    s_out = lax.dynamic_slice_in_dim(s_out, holder_id * share, share, 0)
    factor = 1.0 / math.sqrt(views * holders * images.shape[1] * images.shape[2])
    return (
        (s_kernel * factor).astype(jnp.bfloat16)[None],
        (s_gain * factor).astype(jnp.bfloat16)[None],
        (s_in * factor).astype(jnp.bfloat16)[None],
        (s_out * factor).astype(jnp.bfloat16)[None],
        (s_scale * factor).astype(jnp.bfloat16)[None],
    )


def solution(mesh):
    return jax.shard_map(
        per_device,
        mesh=mesh,
        in_specs=(
            P("dp", None, None, None),
            P("section", None, None),
            P("section", None),
            P("section", None, None),
            P("section", None, None),
            P("section", None),
            P("dp", None, None, None),
            P("dp"),
        ),
        out_specs=(
            P("section", None, None),
            P("section", None),
            P("section", None, "dp"),
            P("section", "dp", None),
            P("section", None),
        ),
        check_vma=False,
    )
```

profile of v0, /device:TPU:448, one launch (start us, length us, event | category | flops | bytes accessed | tf_op | source)
XLA Modules:
  0.0 742.0 jit_solution(8606042368855158967)
XLA Ops:
  15.3 2.8 pad_maximum_fusion
  21.6 150.3 %while.43 = (s32[]{:T(128)}, bf16[12,12,256]{2,1,0:T(8,128)(2,1)S(1)}, bf16[2,12,12,256]{3,2,1,0:T(8,128)(2,1)}, pred[]{:T(512)}, bf16[2,12,12,256]{3,2,1,0:T(8,...) while((s32[]{:T(128)}, ...), condition=%wide.region_3.4_spmd, body=%wide.region_0.3_spmd.sunk | while | flops 164745376 | bytes 3836743 | solution.py:188
  27.9 2.6 fusion.336
  32.6 5.2 collective-permute-done
  44.2 2.6 fusion.336
  48.8 5.2 collective-permute-done
  60.4 2.6 fusion.336
  65.1 5.2 collective-permute-done
  76.6 2.6 fusion.336
  81.3 5.2 collective-permute-done
  92.9 2.6 fusion.336
  97.6 5.2 collective-permute-done
  109.1 2.6 fusion.336
  113.8 5.9 collective-permute-done
  126.0 2.6 fusion.336
  130.7 6.2 collective-permute-done
  143.3 2.6 fusion.336
  148.0 6.6 collective-permute-done
  161.0 2.6 fusion.336
  165.6 6.3 collective-permute-done
  172.5 305.3 %while.44 = (s32[]{:T(128)}, bf16[12,12,256]{2,1,0:T(8,128)(2,1)}, f32[49,256]{1,0:T(8,128)}, f32[256]{0:T(256)}, f32[256,1024]{1,0:T(8,128)S(1)}, /*index=5*/f3...) while((s32[]{:T(128)}, bf16[12,12,256]{2,1,0:T(8,128)(2,1)}, ...), condition=%wide.region_60.61_spmd.clone, body=%wide.region_4.60_spmd.clone.sunk | while | flops 478103168 | bytes 20577308 | solution.py:211
  180.5 2.1 fusion.354
  195.0 2.3 fusion.359
  197.3 5.6 collective-permute-start.1
  216.1 2.1 fusion.354
  230.7 2.3 fusion.359
  233.0 5.3 collective-permute-start.1
  252.2 2.1 fusion.354
  266.7 2.3 fusion.359
  269.0 5.3 collective-permute-start.1
  288.2 2.1 fusion.354
  302.7 2.3 fusion.359
  305.0 2.1 collective-permute-start.1
  321.0 2.1 fusion.354
  335.6 2.3 fusion.359
  337.9 2.8 collective-permute-start.1
  369.0 2.3 fusion.359
  371.3 2.1 collective-permute-start.1
  387.3 2.1 fusion.354
  401.8 2.3 fusion.359
  404.2 2.1 collective-permute-start.1
  420.2 2.1 fusion.354
  434.7 2.3 fusion.359
  437.0 2.1 collective-permute-start.1
  453.0 2.1 fusion.354
  467.5 2.3 fusion.359
  469.8 2.1 collective-permute-start.1
  479.3 251.4 %all-reduce.3 = (f32[49,256]{1,0:T(8,128)S(1)}, f32[256]{0:T(256)S(1)}, f32[256]{0:T(256)S(1)}) all-reduce(f32[49,256]{1,0:T(8,128)S(1)} %copy-done.11, f32[256]{0:T(256)S(1)} %copy-done.88, f32[256]{0:T(256)S(1)} %copy-done.87), channel_id=1, replica_groups=mesh['section'=8,'dp'=64] {'dp'}, use_global_device_ids=true, to_apply=%region_61.62 | all-reduce | flops 13056 | bytes 104448 | tf_op jit(solution)/shard_map/psum | solution.py:214
  (1958 shorter events, 318.8 us)
Async XLA Ops:
  7.2 725.3 %all-reduce.7.cloned.1.call-start = ((), (), s32[]{:S(2)}) async-start(), calls=%async_computation | async-start | bytes 4194304 | tf_op jit(solution)/shard_map/psum | solution.py:214
  7.2 8.1 %collective-permute-start.2 = (bf16[6,12,12,256]{3,2,1,0:T(8,128)(2,1)}, bf16[6,12,12,256]{3,2,1,0:T(8,128)(2,1)S(1)}, u32[]{:S(2)}, u32[]{:S(2)}) collective-permute-start(bf16[6,12,12,256]{3,2,1,0:T(8,128)(2,1)} %param.18), channel_id=1, source_target_pairs={{0,1},{1,2},{2,3},{3,4},{4,5},{5,6},{6,7},{7,8},{8,9},{9,10},{10,1... | collective-permute-start | bytes 1327112 | tf_op jit(solution)/shard_map/ppermute | solution.py:16
  9.0 6.3 collective-permute-start.3
  31.3 6.5 collective-permute-start
  47.5 6.5 collective-permute-start
  63.8 6.5 collective-permute-start
  80.0 6.5 collective-permute-start
  96.3 6.5 collective-permute-start
  112.5 7.2 collective-permute-start
  129.4 7.5 %collective-permute-start = (bf16[12,12,256]{2,1,0:T(8,128)(2,1)S(1)}, bf16[12,12,256]{2,1,0:T(8,128)(2,1)S(1)}, u32[]{:S(2)}, u32[]{:S(2)}) collective-permute-start(bf16[12,12,256]{2,1,0:T(8,128)(2,1)S(1)} %fusion.337), channel_id=1, source_target_pairs={{0,64},{64,128},{128,192},{192,256},{256,320},{320,384},{384,448},... | collective-permute-start | bytes 221192 | tf_op jit(solution)/shard_map/while/body/eval_jaxpr/ppermute | solution.py:27
  146.7 7.9 %collective-permute-start = (bf16[12,12,256]{2,1,0:T(8,128)(2,1)S(1)}, bf16[12,12,256]{2,1,0:T(8,128)(2,1)S(1)}, u32[]{:S(2)}, u32[]{:S(2)}) collective-permute-start(bf16[12,12,256]{2,1,0:T(8,128)(2,1)S(1)} %fusion.337), channel_id=1, source_target_pairs={{0,64},{64,128},{128,192},{192,256},{256,320},{320,384},{384,448},... | collective-permute-start | bytes 221192 | tf_op jit(solution)/shard_map/while/body/eval_jaxpr/ppermute | solution.py:27
  164.3 7.6 %collective-permute-start = (bf16[12,12,256]{2,1,0:T(8,128)(2,1)S(1)}, bf16[12,12,256]{2,1,0:T(8,128)(2,1)S(1)}, u32[]{:S(2)}, u32[]{:S(2)}) collective-permute-start(bf16[12,12,256]{2,1,0:T(8,128)(2,1)S(1)} %fusion.337), channel_id=1, source_target_pairs={{0,64},{64,128},{128,192},{192,256},{256,320},{320,384},{384,448},... | collective-permute-start | bytes 221192 | tf_op jit(solution)/shard_map/while/body/eval_jaxpr/ppermute | solution.py:27
  172.6 10.0 %copy-start.3 = (bf16[256,1024]{1,0:T(8,128)(2,1)}, bf16[256,1024]{1,0:T(8,128)(2,1)S(1)}, u32[]{:S(2)}) copy-start(bf16[256,1024]{1,0:T(8,128)(2,1)S(1)} %get-tuple-element.1509) | copy-start | bytes 1572868 | tf_op jit(solution)/shard_map/while
  173.6 9.0 %copy-start.14 = (f32[1,256]{1,0:T(1,128)}, f32[1,256]{1,0:T(1,128)S(1)}, u32[]{:S(2)}) copy-start(f32[1,256]{1,0:T(1,128)S(1)} %get-tuple-element.1349) | copy-start | bytes 3076 | tf_op jit(solution)/shard_map/while
  173.6 9.0 %copy-start.15 = (f32[1,256]{1,0:T(1,128)}, f32[1,256]{1,0:T(1,128)S(1)}, u32[]{:S(2)}) copy-start(f32[1,256]{1,0:T(1,128)S(1)} %get-tuple-element.1339) | copy-start | bytes 3076 | tf_op jit(solution)/shard_map/while
  197.3 10.4 %collective-permute-start.1 = (bf16[12,12,256]{2,1,0:T(8,128)(2,1)S(1)}, bf16[12,12,256]{2,1,0:T(8,128)(2,1)}, u32[]{:S(2)}, u32[]{:S(2)}) collective-permute-start(bf16[12,12,256]{2,1,0:T(8,128)(2,1)S(1)} %fusion.359), channel_id=1, source_target_pairs={{64,0},{128,64},{192,128},{256,192},{320,256},{384,320},{448,384},... | collective-permute-start | bytes 221192 | tf_op jit(solution)/shard_map/while/body/eval_jaxpr/ppermute | solution.py:27
  208.2 10.0 %copy-start.3 = (bf16[256,1024]{1,0:T(8,128)(2,1)}, bf16[256,1024]{1,0:T(8,128)(2,1)S(1)}, u32[]{:S(2)}) copy-start(bf16[256,1024]{1,0:T(8,128)(2,1)S(1)} %get-tuple-element.1509) | copy-start | bytes 1572868 | tf_op jit(solution)/shard_map/while
  209.3 9.0 %copy-start.14 = (f32[1,256]{1,0:T(1,128)}, f32[1,256]{1,0:T(1,128)S(1)}, u32[]{:S(2)}) copy-start(f32[1,256]{1,0:T(1,128)S(1)} %get-tuple-element.1349) | copy-start | bytes 3076 | tf_op jit(solution)/shard_map/while
  209.3 9.0 %copy-start.15 = (f32[1,256]{1,0:T(1,128)}, f32[1,256]{1,0:T(1,128)S(1)}, u32[]{:S(2)}) copy-start(f32[1,256]{1,0:T(1,128)S(1)} %get-tuple-element.1339) | copy-start | bytes 3076 | tf_op jit(solution)/shard_map/while
  233.0 10.7 %collective-permute-start.1 = (bf16[12,12,256]{2,1,0:T(8,128)(2,1)S(1)}, bf16[12,12,256]{2,1,0:T(8,128)(2,1)}, u32[]{:S(2)}, u32[]{:S(2)}) collective-permute-start(bf16[12,12,256]{2,1,0:T(8,128)(2,1)S(1)} %fusion.359), channel_id=1, source_target_pairs={{64,0},{128,64},{192,128},{256,192},{320,256},{384,320},{448,384},... | collective-permute-start | bytes 221192 | tf_op jit(solution)/shard_map/while/body/eval_jaxpr/ppermute | solution.py:27
  244.3 10.0 %copy-start.3 = (bf16[256,1024]{1,0:T(8,128)(2,1)}, bf16[256,1024]{1,0:T(8,128)(2,1)S(1)}, u32[]{:S(2)}) copy-start(bf16[256,1024]{1,0:T(8,128)(2,1)S(1)} %get-tuple-element.1509) | copy-start | bytes 1572868 | tf_op jit(solution)/shard_map/while
  245.3 9.0 %copy-start.14 = (f32[1,256]{1,0:T(1,128)}, f32[1,256]{1,0:T(1,128)S(1)}, u32[]{:S(2)}) copy-start(f32[1,256]{1,0:T(1,128)S(1)} %get-tuple-element.1349) | copy-start | bytes 3076 | tf_op jit(solution)/shard_map/while
  245.3 9.0 %copy-start.15 = (f32[1,256]{1,0:T(1,128)}, f32[1,256]{1,0:T(1,128)S(1)}, u32[]{:S(2)}) copy-start(f32[1,256]{1,0:T(1,128)S(1)} %get-tuple-element.1339) | copy-start | bytes 3076 | tf_op jit(solution)/shard_map/while
  269.0 10.7 %collective-permute-start.1 = (bf16[12,12,256]{2,1,0:T(8,128)(2,1)S(1)}, bf16[12,12,256]{2,1,0:T(8,128)(2,1)}, u32[]{:S(2)}, u32[]{:S(2)}) collective-permute-start(bf16[12,12,256]{2,1,0:T(8,128)(2,1)S(1)} %fusion.359), channel_id=1, source_target_pairs={{64,0},{128,64},{192,128},{256,192},{320,256},{384,320},{448,384},... | collective-permute-start | bytes 221192 | tf_op jit(solution)/shard_map/while/body/eval_jaxpr/ppermute | solution.py:27
  280.3 10.0 %copy-start.3 = (bf16[256,1024]{1,0:T(8,128)(2,1)}, bf16[256,1024]{1,0:T(8,128)(2,1)S(1)}, u32[]{:S(2)}) copy-start(bf16[256,1024]{1,0:T(8,128)(2,1)S(1)} %get-tuple-element.1509) | copy-start | bytes 1572868 | tf_op jit(solution)/shard_map/while
  281.4 9.0 %copy-start.14 = (f32[1,256]{1,0:T(1,128)}, f32[1,256]{1,0:T(1,128)S(1)}, u32[]{:S(2)}) copy-start(f32[1,256]{1,0:T(1,128)S(1)} %get-tuple-element.1349) | copy-start | bytes 3076 | tf_op jit(solution)/shard_map/while
  281.4 9.0 %copy-start.15 = (f32[1,256]{1,0:T(1,128)}, f32[1,256]{1,0:T(1,128)S(1)}, u32[]{:S(2)}) copy-start(f32[1,256]{1,0:T(1,128)S(1)} %get-tuple-element.1339) | copy-start | bytes 3076 | tf_op jit(solution)/shard_map/while
  305.0 7.5 %collective-permute-start.1 = (bf16[12,12,256]{2,1,0:T(8,128)(2,1)S(1)}, bf16[12,12,256]{2,1,0:T(8,128)(2,1)}, u32[]{:S(2)}, u32[]{:S(2)}) collective-permute-start(bf16[12,12,256]{2,1,0:T(8,128)(2,1)S(1)} %fusion.359), channel_id=1, source_target_pairs={{64,0},{128,64},{192,128},{256,192},{320,256},{384,320},{448,384},... | collective-permute-start | bytes 221192 | tf_op jit(solution)/shard_map/while/body/eval_jaxpr/ppermute | solution.py:27
  313.1 10.0 %copy-start.3 = (bf16[256,1024]{1,0:T(8,128)(2,1)}, bf16[256,1024]{1,0:T(8,128)(2,1)S(1)}, u32[]{:S(2)}) copy-start(bf16[256,1024]{1,0:T(8,128)(2,1)S(1)} %get-tuple-element.1509) | copy-start | bytes 1572868 | tf_op jit(solution)/shard_map/while
  314.2 9.0 %copy-start.14 = (f32[1,256]{1,0:T(1,128)}, f32[1,256]{1,0:T(1,128)S(1)}, u32[]{:S(2)}) copy-start(f32[1,256]{1,0:T(1,128)S(1)} %get-tuple-element.1349) | copy-start | bytes 3076 | tf_op jit(solution)/shard_map/while
  314.2 9.0 %copy-start.15 = (f32[1,256]{1,0:T(1,128)}, f32[1,256]{1,0:T(1,128)S(1)}, u32[]{:S(2)}) copy-start(f32[1,256]{1,0:T(1,128)S(1)} %get-tuple-element.1339) | copy-start | bytes 3076 | tf_op jit(solution)/shard_map/while
  337.9 8.2 %collective-permute-start.1 = (bf16[12,12,256]{2,1,0:T(8,128)(2,1)S(1)}, bf16[12,12,256]{2,1,0:T(8,128)(2,1)}, u32[]{:S(2)}, u32[]{:S(2)}) collective-permute-start(bf16[12,12,256]{2,1,0:T(8,128)(2,1)S(1)} %fusion.359), channel_id=1, source_target_pairs={{64,0},{128,64},{192,128},{256,192},{320,256},{384,320},{448,384},... | collective-permute-start | bytes 221192 | tf_op jit(solution)/shard_map/while/body/eval_jaxpr/ppermute | solution.py:27
  346.6 10.0 %copy-start.3 = (bf16[256,1024]{1,0:T(8,128)(2,1)}, bf16[256,1024]{1,0:T(8,128)(2,1)S(1)}, u32[]{:S(2)}) copy-start(bf16[256,1024]{1,0:T(8,128)(2,1)S(1)} %get-tuple-element.1509) | copy-start | bytes 1572868 | tf_op jit(solution)/shard_map/while
  347.6 9.0 %copy-start.14 = (f32[1,256]{1,0:T(1,128)}, f32[1,256]{1,0:T(1,128)S(1)}, u32[]{:S(2)}) copy-start(f32[1,256]{1,0:T(1,128)S(1)} %get-tuple-element.1349) | copy-start | bytes 3076 | tf_op jit(solution)/shard_map/while
  347.7 9.0 %copy-start.15 = (f32[1,256]{1,0:T(1,128)}, f32[1,256]{1,0:T(1,128)S(1)}, u32[]{:S(2)}) copy-start(f32[1,256]{1,0:T(1,128)S(1)} %get-tuple-element.1339) | copy-start | bytes 3076 | tf_op jit(solution)/shard_map/while
  371.3 7.5 %collective-permute-start.1 = (bf16[12,12,256]{2,1,0:T(8,128)(2,1)S(1)}, bf16[12,12,256]{2,1,0:T(8,128)(2,1)}, u32[]{:S(2)}, u32[]{:S(2)}) collective-permute-start(bf16[12,12,256]{2,1,0:T(8,128)(2,1)S(1)} %fusion.359), channel_id=1, source_target_pairs={{64,0},{128,64},{192,128},{256,192},{320,256},{384,320},{448,384},... | collective-permute-start | bytes 221192 | tf_op jit(solution)/shard_map/while/body/eval_jaxpr/ppermute | solution.py:27
  379.4 10.0 %copy-start.3 = (bf16[256,1024]{1,0:T(8,128)(2,1)}, bf16[256,1024]{1,0:T(8,128)(2,1)S(1)}, u32[]{:S(2)}) copy-start(bf16[256,1024]{1,0:T(8,128)(2,1)S(1)} %get-tuple-element.1509) | copy-start | bytes 1572868 | tf_op jit(solution)/shard_map/while
  380.5 9.0 %copy-start.14 = (f32[1,256]{1,0:T(1,128)}, f32[1,256]{1,0:T(1,128)S(1)}, u32[]{:S(2)}) copy-start(f32[1,256]{1,0:T(1,128)S(1)} %get-tuple-element.1349) | copy-start | bytes 3076 | tf_op jit(solution)/shard_map/while
  380.5 9.0 %copy-start.15 = (f32[1,256]{1,0:T(1,128)}, f32[1,256]{1,0:T(1,128)S(1)}, u32[]{:S(2)}) copy-start(f32[1,256]{1,0:T(1,128)S(1)} %get-tuple-element.1339) | copy-start | bytes 3076 | tf_op jit(solution)/shard_map/while
  404.2 7.5 %collective-permute-start.1 = (bf16[12,12,256]{2,1,0:T(8,128)(2,1)S(1)}, bf16[12,12,256]{2,1,0:T(8,128)(2,1)}, u32[]{:S(2)}, u32[]{:S(2)}) collective-permute-start(bf16[12,12,256]{2,1,0:T(8,128)(2,1)S(1)} %fusion.359), channel_id=1, source_target_pairs={{64,0},{128,64},{192,128},{256,192},{320,256},{384,320},{448,384},... | collective-permute-start | bytes 221192 | tf_op jit(solution)/shard_map/while/body/eval_jaxpr/ppermute | solution.py:27
  412.2 10.0 %copy-start.3 = (bf16[256,1024]{1,0:T(8,128)(2,1)}, bf16[256,1024]{1,0:T(8,128)(2,1)S(1)}, u32[]{:S(2)}) copy-start(bf16[256,1024]{1,0:T(8,128)(2,1)S(1)} %get-tuple-element.1509) | copy-start | bytes 1572868 | tf_op jit(solution)/shard_map/while
  413.3 9.0 %copy-start.14 = (f32[1,256]{1,0:T(1,128)}, f32[1,256]{1,0:T(1,128)S(1)}, u32[]{:S(2)}) copy-start(f32[1,256]{1,0:T(1,128)S(1)} %get-tuple-element.1349) | copy-start | bytes 3076 | tf_op jit(solution)/shard_map/while
  413.3 9.0 %copy-start.15 = (f32[1,256]{1,0:T(1,128)}, f32[1,256]{1,0:T(1,128)S(1)}, u32[]{:S(2)}) copy-start(f32[1,256]{1,0:T(1,128)S(1)} %get-tuple-element.1339) | copy-start | bytes 3076 | tf_op jit(solution)/shard_map/while
  437.0 7.5 %collective-permute-start.1 = (bf16[12,12,256]{2,1,0:T(8,128)(2,1)S(1)}, bf16[12,12,256]{2,1,0:T(8,128)(2,1)}, u32[]{:S(2)}, u32[]{:S(2)}) collective-permute-start(bf16[12,12,256]{2,1,0:T(8,128)(2,1)S(1)} %fusion.359), channel_id=1, source_target_pairs={{64,0},{128,64},{192,128},{256,192},{320,256},{384,320},{448,384},... | collective-permute-start | bytes 221192 | tf_op jit(solution)/shard_map/while/body/eval_jaxpr/ppermute | solution.py:27
  445.1 10.0 %copy-start.3 = (bf16[256,1024]{1,0:T(8,128)(2,1)}, bf16[256,1024]{1,0:T(8,128)(2,1)S(1)}, u32[]{:S(2)}) copy-start(bf16[256,1024]{1,0:T(8,128)(2,1)S(1)} %get-tuple-element.1509) | copy-start | bytes 1572868 | tf_op jit(solution)/shard_map/while
  446.1 9.0 %copy-start.14 = (f32[1,256]{1,0:T(1,128)}, f32[1,256]{1,0:T(1,128)S(1)}, u32[]{:S(2)}) copy-start(f32[1,256]{1,0:T(1,128)S(1)} %get-tuple-element.1349) | copy-start | bytes 3076 | tf_op jit(solution)/shard_map/while
  446.1 9.0 %copy-start.15 = (f32[1,256]{1,0:T(1,128)}, f32[1,256]{1,0:T(1,128)S(1)}, u32[]{:S(2)}) copy-start(f32[1,256]{1,0:T(1,128)S(1)} %get-tuple-element.1339) | copy-start | bytes 3076 | tf_op jit(solution)/shard_map/while
  469.8 7.5 %collective-permute-start.1 = (bf16[12,12,256]{2,1,0:T(8,128)(2,1)S(1)}, bf16[12,12,256]{2,1,0:T(8,128)(2,1)}, u32[]{:S(2)}, u32[]{:S(2)}) collective-permute-start(bf16[12,12,256]{2,1,0:T(8,128)(2,1)S(1)} %fusion.359), channel_id=1, source_target_pairs={{64,0},{128,64},{192,128},{256,192},{320,256},{384,320},{448,384},... | collective-permute-start | bytes 221192 | tf_op jit(solution)/shard_map/while/body/eval_jaxpr/ppermute | solution.py:27
  (734 other events, 3010.3 us)
Sparse Core Ops, SparseCore 0:
  479.4 206.1 all-reduce.6
where the time goes:
time: 750 us; the launch traced here: 742 us
  blocking collectives  251 us (33%)
  other arithmetic  178 us (24%)
  local copies, waits for them, and re-layouts  98.9 us (13%)
  matrix products  90.6 us (12%)
  waiting for transfers between devices  51.1 us (7%)
  starting transfers between devices  44.4 us (6%)
  between operations  14.2 us (2%)
  loops' own time  12.9 us (2%)
    psum x1, blocking collectives, per_device(): lax.psum((g_kernel, norm_gain_gradient, g_in, g_out, g_scale), 'dp')  251 us
    slice x54, local copies, waits for them, and re-layouts, depthwise(): kernel[row_tap * ksize + col_tap]  60.2 us
    ppermute x18, waiting for transfers between devices, from_behind(): return lax.ppermute(block, axis, route)  51.1 us
    ppermute x18, starting transfers between devices, from_behind(): return lax.ppermute(block, axis, route)  41.3 us
    reduce_sum x27, other arithmetic, block_backward(): kernel_rows.append(jnp.sum(depthwise_cotangent * window, axis=(0, 1, 2)))  37.1 us
    dot_general x18, matrix products, block_forward(): jnp.dot(hidden_expanded, proj_out, preferred_element_type=jnp.float32)  35.4 us
    reduce_sum x18, other arithmetic, block_forward(): centered_input = jnp.mean(depthwise_output, axis=-1, keepdims=True)  30.7 us
    while x1512, local copies, waits for them, and re-layouts  23.1 us
  transfers between devices with their start and end apart: 21, of which 9 were waited for; matrix products, arithmetic and copies ran while one was open for 6% of the time, Pallas kernels for 0%

commit v1 on v0

--- a/solution.py
+++ b/solution.py
@@ -74,9 +74,8 @@
     )
 
 
-def block_backward(inputs, params, arrived, ksize):
+def block_backward(inputs, params, arrived, ksize, saved_residuals):
     kernel, norm_gain, proj_in, proj_out, scale = params
-    _, saved_residuals = block_forward(inputs, params, ksize)
     (
         standardized_input,
         inverse_deviation,
@@ -140,6 +139,38 @@
     return (ct_inputs.astype(jnp.bfloat16), (g_kernel, norm_gain_gradient, g_in, g_out, g_scale))
 
 
+def dp_reduce(g_in, g_out, small, axis):
+    holders = lax.axis_size(axis)
+    bits = holders.bit_length() - 1
+    assert 1 << bits == holders
+    me = lax.axis_index(axis)
+    channels, hidden = g_in.shape
+    share = hidden // holders
+    blocks_in = g_in.reshape(channels, holders, share).transpose(1, 0, 2).reshape(holders, -1)
+    blocks_out = g_out.reshape(holders, share * channels)
+    big = jnp.concatenate([blocks_in, blocks_out], axis=1)
+    width = big.shape[1]
+    big = big.reshape((2,) * bits + (width,))
+    remaining = list(range(bits - 1, -1, -1))
+    order = [0] + [b for b in (1, 4, 2, 5, 3) if b < bits] + [b for b in range(6, bits)]
+    for bit in order:
+        position = remaining.index(bit)
+        mine = (me >> bit) & 1
+        keep = lax.dynamic_index_in_dim(big, mine, position, keepdims=False)
+        send = lax.dynamic_index_in_dim(big, 1 - mine, position, keepdims=False)
+        shape = keep.shape
+        packet = jnp.concatenate([send.reshape(-1), small])
+        pairs = [(d, d ^ (1 << bit)) for d in range(holders)]
+        got = lax.ppermute(packet, axis, pairs)
+        big = keep + got[: keep.size].reshape(shape)
+        small = small + got[keep.size :]
+        remaining.pop(position)
+    big = big.reshape(width)
+    s_in = big[: channels * share].reshape(channels, share)
+    s_out = big[channels * share :].reshape(share, channels)
+    return s_in, s_out, small
+
+
 def per_device(images, dw_kernel, ln_gain, w_in, w_out, layer_scale, scene_grad, view_slot):
     section_id = lax.axis_index("section")
     sections = lax.axis_size("section")
@@ -165,30 +196,39 @@
     empty_map = jnp.zeros(images.shape[1:], jnp.bfloat16)
 
     def run_block(current):
-        return block_forward(current[None], params, ksize)[0][0]
+        out, res = block_forward(current[None], params, ksize)
+        return out[0], res
+
+    probe = jax.eval_shape(run_block, empty_map)[1]
+    start_store = (
+        jnp.zeros((views + 1,) + images.shape[1:], images.dtype),
+        jax.tree.map(lambda r: jnp.zeros((views + 1,) + r.shape, r.dtype), probe),
+    )
 
     def forward_tick(tick, carry):
-        incoming, saved_residuals = carry
+        incoming, store = carry
         micro = tick - section_id
         valid = (micro >= 0) & (micro < views)
-        index = jnp.clip(micro, 0, views - 1)
+        index = jnp.where(valid, micro, views)
         own_image = lax.dynamic_index_in_dim(
             images, jnp.clip(tick, 0, views - 1), 0, keepdims=False
         )
         current = jnp.where(section_id == 0, own_image, incoming)
-        saved_residuals = jnp.where(
-            valid,
-            lax.dynamic_update_index_in_dim(saved_residuals, current, index, 0),
-            saved_residuals,
-        )
-        result = run_block(current)
+        result, res = run_block(current)
         incoming = from_behind(result, "section", 1)
-        return (incoming, saved_residuals)
-
-    _, saved_residuals = lax.fori_loop(0, ticks, forward_tick, (empty_map, jnp.zeros_like(images)))
-
-    def backward_step(current, arrived):
-        back_x, back_p = block_backward(current[None], params, arrived[None], ksize)
+        store = jax.tree.map(
+            lambda buf, val: lax.dynamic_update_index_in_dim(buf, val, index, 0),
+            store,
+            (current, res),
+        )
+        return (incoming, store)
+
+    _, (saved_inputs, saved_res) = lax.fori_loop(
+        0, ticks, forward_tick, (empty_map, start_store)
+    )
+
+    def backward_step(current, arrived, res):
+        back_x, back_p = block_backward(current[None], params, arrived[None], ksize, res)
         return (back_x[0], back_p)
 
     start_totals = jax.tree.map(lambda member: jnp.zeros(member.shape, jnp.float32), params)
@@ -200,8 +240,11 @@
         index = jnp.clip(micro, 0, views - 1)
         own_target = lax.dynamic_index_in_dim(targets, index, 0, keepdims=False)
         arrived = jnp.where(section_id == sections - 1, own_target, incoming)
-        current = lax.dynamic_index_in_dim(saved_residuals, index, 0, keepdims=False)
-        back_x, back_p = backward_step(current, arrived)
+        current = lax.dynamic_index_in_dim(saved_inputs, index, 0, keepdims=False)
+        res = jax.tree.map(
+            lambda buf: lax.dynamic_index_in_dim(buf, index, 0, keepdims=False), saved_res
+        )
+        back_x, back_p = backward_step(current, arrived, res)
         totals = jax.tree.map(
             lambda total, term: total + jnp.where(valid, term, 0.0), totals, back_p
         )
@@ -210,12 +253,15 @@
 
     _, totals = lax.fori_loop(0, ticks, backward_tick, (empty_map, start_totals))
     g_kernel, norm_gain_gradient, g_in, g_out, g_scale = totals
-    share = g_in.shape[1] // holders
-    s_kernel, s_gain, s_in, s_out, s_scale = lax.psum(
-        (g_kernel, norm_gain_gradient, g_in, g_out, g_scale), "dp"
-    )
-    s_in = lax.dynamic_slice_in_dim(s_in, holder_id * share, share, 1)
-    s_out = lax.dynamic_slice_in_dim(s_out, holder_id * share, share, 0)
+    small = jnp.concatenate(
+        [g_kernel.reshape(-1), norm_gain_gradient.reshape(-1), g_scale.reshape(-1)]
+    )
+    s_in, s_out, small = dp_reduce(g_in, g_out, small, "dp")
+    n_kernel = g_kernel.size
+    n_gain = norm_gain_gradient.size
+    s_kernel = small[:n_kernel].reshape(g_kernel.shape)
+    s_gain = small[n_kernel : n_kernel + n_gain].reshape(norm_gain_gradient.shape)
+    s_scale = small[n_kernel + n_gain :].reshape(g_scale.shape)
     factor = 1.0 / math.sqrt(views * holders * images.shape[1] * images.shape[2])
     return (
         (s_kernel * factor).astype(jnp.bfloat16)[None],

time: 750 us -> 472 us (0.63)
  blocking collectives: 251 us -> 0 us
  starting transfers between devices: 44.4 us -> 74.1 us
  other arithmetic: 178 us -> 161 us
  matrix products: 90.6 us -> 75.4 us
  between operations: 14.2 us -> 1.14 us
  local copies, waits for them, and re-layouts: 98.9 us -> 86.2 us
  waiting for transfers between devices: 51.1 us -> 63.3 us
    psum x1 -> x0, blocking collectives: 251 us -> none  [per_device(): lax.psum((g_kernel, norm_gain_gradient, g_in, g_out, g_scale), 'dp')]
    slice x54 -> x27, local copies, waits for them, and re-layouts: 60.2 us -> 0.4 us  [depthwise(): kernel[row_tap * ksize + col_tap]]
    dynamic_update_slice x0 -> x36, other arithmetic: none -> 45.8 us  [forward_tick(): lax.dynamic_update_index_in_dim(buf, val, index, 0)]
    ppermute x0 -> x6, waiting for transfers between devices: none -> 37.8 us  [dp_reduce(): got = lax.ppermute(packet, axis, pairs)]
    dot_general x18 -> x9, matrix products: 35.4 us -> 2.17 us  [block_forward(): jnp.dot(hidden_expanded, proj_out, preferred_element_type=jnp.float32)]
    ppermute x0 -> x6, starting transfers between devices: none -> 30.1 us  [dp_reduce(): got = lax.ppermute(packet, axis, pairs)]
    ppermute x18, waiting for transfers between devices: 51.1 us -> 25.5 us  [from_behind(): return lax.ppermute(block, axis, route)]
    reduce_sum x18 -> x9, other arithmetic: 30.7 us -> 12.2 us  [block_forward(): centered_input = jnp.mean(depthwise_output, axis=-1, keepdims=True)]
  transfers between devices with their start and end apart: 21 -> 26, of which waited for: 9 -> 15; matrix products, arithmetic and copies ran while one was open for 6% -> 16% of each run, Pallas kernels for 0% -> 0%
where the time goes in v1:
time: 472 us; the launch traced here: 467 us
  other arithmetic  161 us (34%)
  local copies, waits for them, and re-layouts  86.2 us (18%)
  matrix products  75.4 us (16%)
  starting transfers between devices  74.1 us (16%)
  waiting for transfers between devices  63.3 us (13%)
  loops' own time  5.47 us (1%)
    dynamic_update_slice x36, other arithmetic, forward_tick(): lax.dynamic_update_index_in_dim(buf, val, index, 0)  45.8 us
    ppermute x18, starting transfers between devices, from_behind(): return lax.ppermute(block, axis, route)  41 us
    ppermute x6, waiting for transfers between devices, dp_reduce(): got = lax.ppermute(packet, axis, pairs)  37.8 us
    ppermute x6, starting transfers between devices, dp_reduce(): got = lax.ppermute(packet, axis, pairs)  30.1 us
    dot_general x9, matrix products, block_forward(): jnp.dot(normalized_input.reshape(-1, channels), proj_in, preferred_elemen...  29 us
    ppermute x18, waiting for transfers between devices, from_behind(): return lax.ppermute(block, axis, route)  25.5 us
    reduce_sum x27, other arithmetic, block_backward(): kernel_rows.append(jnp.sum(depthwise_cotangent * window, axis=(0, 1, 2)))  25.1 us
    squeeze x9, other arithmetic, backward_step(): return (back_x[0], back_p)  18.4 us
  transfers between devices with their start and end apart: 26, of which 15 were waited for; matrix products, arithmetic and copies ran while one was open for 16% of the time, Pallas kernels for 0%

profile of v1, /device:TPU:448, one launch (start us, length us, event | category | flops | bytes accessed | tf_op | source)
XLA Modules:
  0.0 466.7 jit_solution(12212442897081152655)
XLA Ops:
  9.4 2.5 pad_maximum_fusion
  21.0 144.5 %while.55 = (s32[]{:T(128)}, bf16[12,12,256]{2,1,0:T(8,128)(2,1)S(1)}, bf16[3,12,12,256]{3,2,1,0:T(8,128)(2,1)}, f32[3,1,12,12,256]{4,3,2,1,0:T(8,128)}, f32[3,1...) while((s32[]{:T(128)}, ...), condition=%wide.region_3.4_spmd, body=%wide.region_0.3_spmd.sunk | while | flops 164782528 | bytes 9619837 | solution.py:226
  25.7 3.2 bitcast_dynamic-update-slice_fusion.14
  34.2 2.4 collective-permute-done
  41.4 3.2 bitcast_dynamic-update-slice_fusion.14
  49.9 2.4 collective-permute-done
  57.0 3.2 bitcast_dynamic-update-slice_fusion.14
  65.5 2.4 collective-permute-done
  72.6 3.2 bitcast_dynamic-update-slice_fusion.14
  81.1 2.4 collective-permute-done
  88.2 3.2 bitcast_dynamic-update-slice_fusion.14
  96.7 2.7 collective-permute-done
  104.2 3.2 bitcast_dynamic-update-slice_fusion.14
  112.6 3.0 collective-permute-done
  120.4 3.2 bitcast_dynamic-update-slice_fusion.14
  128.9 3.3 collective-permute-done
  136.9 3.2 bitcast_dynamic-update-slice_fusion.14
  145.4 3.9 collective-permute-done
  154.0 3.2 bitcast_dynamic-update-slice_fusion.14
  162.5 3.0 collective-permute-done
  165.5 202.3 %while.56 = (s32[]{:T(128)}, bf16[12,12,256]{2,1,0:T(8,128)(2,1)S(1)}, f32[49,256]{1,0:T(8,128)S(1)}, f32[256]{0:T(256)}, f32[256,1024]{1,0:T(8,128)S(1)}, /*ind...) while((s32[]{:T(128)}, ...), condition=%wide.region_58.59_spmd.clone, body=%wide.region_4.58_spmd.clone.sunk | while | flops 313505280 | bytes 12293400 | solution.py:254
  177.3 2.0 fusion.415
  179.4 5.1 %collective-permute-start.1 = (bf16[12,12,256]{2,1,0:T(8,128)(2,1)S(1)}, bf16[12,12,256]{2,1,0:T(8,128)(2,1)S(1)}, u32[]{:S(2)}, u32[]{:S(2)}) collective-permute-start(bf16[12,12,256]{2,1,0:T(8,128)(2,1)S(1)} %fusion.415), channel_id=1, source_target_pairs={{64,0},{128,64},{192,128},{256,192},{320,256},{384,320},{448,384},... | collective-permute-start | bytes 221192 | tf_op jit(solution)/shard_map/while/body/eval_jaxpr/ppermute | solution.py:27
  201.6 2.0 fusion.415
  203.6 5.1 %collective-permute-start.1 = (bf16[12,12,256]{2,1,0:T(8,128)(2,1)S(1)}, bf16[12,12,256]{2,1,0:T(8,128)(2,1)S(1)}, u32[]{:S(2)}, u32[]{:S(2)}) collective-permute-start(bf16[12,12,256]{2,1,0:T(8,128)(2,1)S(1)} %fusion.415), channel_id=1, source_target_pairs={{64,0},{128,64},{192,128},{256,192},{320,256},{384,320},{448,384},... | collective-permute-start | bytes 221192 | tf_op jit(solution)/shard_map/while/body/eval_jaxpr/ppermute | solution.py:27
  225.9 2.0 fusion.415
  228.0 5.1 %collective-permute-start.1 = (bf16[12,12,256]{2,1,0:T(8,128)(2,1)S(1)}, bf16[12,12,256]{2,1,0:T(8,128)(2,1)S(1)}, u32[]{:S(2)}, u32[]{:S(2)}) collective-permute-start(bf16[12,12,256]{2,1,0:T(8,128)(2,1)S(1)} %fusion.415), channel_id=1, source_target_pairs={{64,0},{128,64},{192,128},{256,192},{320,256},{384,320},{448,384},... | collective-permute-start | bytes 221192 | tf_op jit(solution)/shard_map/while/body/eval_jaxpr/ppermute | solution.py:27
  250.3 2.0 fusion.415
  252.3 2.2 collective-permute-start.1
  273.7 2.4 collective-permute-start.1
  295.3 2.4 collective-permute-start.1
  316.9 2.4 collective-permute-start.1
  338.4 2.4 collective-permute-start.1
  360.0 2.4 collective-permute-start.1
  368.1 4.6 copy.22
  372.7 7.7 %concatenate.35 = f32[2,2,2,2,2,2,4096]{6,5,4,3,2,1,0:T(2,128)} reshape(f32[64,256,16]{2,1,0:T(8,128)} %copy.22) | data formatting | bytes 2097152 | tf_op jit(solution)/shard_map/concatenate | solution.py:151
  384.8 2.2 constant_dynamic-slice_fusion.9
  389.0 2.8 collective-permute-done.4
  396.8 8.0 %collective-permute-start.5 = (f32[144128]{0:T(1024)S(1)}, f32[144128]{0:T(1024)S(1)}, u32[]{:S(2)}, u32[]{:S(2)}) collective-permute-start(f32[144128]{0:T(1024)S(1)} %pad_maximum_fusion.2), channel_id=1, source_target_pairs={{0,2},{1,3},{2,0},{3,1},{4,6},{5,7},{6,4},{7,5},{8,10},{9,11},{10,... | collective-permute-start | bytes 1729544 | tf_op jit(solution)/shard_map/ppermute | solution.py:164
  404.8 13.3 %collective-permute-done.5 = f32[144128]{0:T(1024)S(1)} collective-permute-done((f32[144128]{0:T(1024)S(1)}, f32[144128]{0:T(1024)S(1)}, u32[]{:S(2)}, u32[]{:S(2)}) %collective-permute-start.5) | collective-permute-done | bytes 576544 | tf_op jit(solution)/shard_map/ppermute | solution.py:164
  419.2 4.7 %collective-permute-start.6 = (f32[78592]{0:T(1024)S(1)}, f32[78592]{0:T(1024)S(1)}, u32[]{:S(2)}, u32[]{:S(2)}) collective-permute-start(f32[78592]{0:T(1024)S(1)} %pad_maximum_fusion.3), channel_id=1, source_target_pairs={{0,16},{1,17},{2,18},{3,19},{4,20},{5,21},{6,22},{7,23},{8,24},{9,... | collective-permute-start | bytes 943112 | tf_op jit(solution)/shard_map/ppermute | solution.py:164
  423.9 6.9 %collective-permute-done.6 = f32[78592]{0:T(1024)S(1)} collective-permute-done((f32[78592]{0:T(1024)S(1)}, f32[78592]{0:T(1024)S(1)}, u32[]{:S(2)}, u32[]{:S(2)}) %collective-permute-start.6) | collective-permute-done | bytes 314400 | tf_op jit(solution)/shard_map/ppermute | solution.py:164
  431.4 3.6 collective-permute-start.7
  435.0 8.2 %collective-permute-done.7 = f32[45824]{0:T(1024)S(1)} collective-permute-done((f32[45824]{0:T(1024)S(1)}, f32[45824]{0:T(1024)S(1)}, u32[]{:S(2)}, u32[]{:S(2)}) %collective-permute-start.7) | collective-permute-done | bytes 183328 | tf_op jit(solution)/shard_map/ppermute | solution.py:164
  443.5 4.9 %collective-permute-start.8 = (f32[29440]{0:T(1024)S(1)}, f32[29440]{0:T(1024)S(1)}, u32[]{:S(2)}, u32[]{:S(2)}) collective-permute-start(f32[29440]{0:T(1024)S(1)} %pad_maximum_fusion.5), channel_id=1, source_target_pairs={{0,32},{1,33},{2,34},{3,35},{4,36},{5,37},{6,38},{7,39},{8,40},{9,... | collective-permute-start | bytes 353288 | tf_op jit(solution)/shard_map/ppermute | solution.py:164
  448.4 3.3 collective-permute-done.8
  453.2 6.9 %collective-permute-start.9 = (f32[21248]{0:T(1024)S(1)}, f32[21248]{0:T(1024)S(1)}, u32[]{:S(2)}, u32[]{:S(2)}) collective-permute-start(f32[21248]{0:T(1024)S(1)} %pad_maximum_fusion.6), channel_id=1, source_target_pairs={{0,8},{1,9},{2,10},{3,11},{4,12},{5,13},{6,14},{7,15},{8,0},{9,1},... | collective-permute-start | bytes 254984 | tf_op jit(solution)/shard_map/ppermute | solution.py:164
  460.2 3.2 collective-permute-done.9
  (962 shorter events, 285.0 us)
Async XLA Ops:
  0.6 8.7 %collective-permute-start.2 = (bf16[6,12,12,256]{3,2,1,0:T(8,128)(2,1)}, bf16[6,12,12,256]{3,2,1,0:T(8,128)(2,1)S(1)}, u32[]{:S(2)}, u32[]{:S(2)}) collective-permute-start(bf16[6,12,12,256]{3,2,1,0:T(8,128)(2,1)} %param.18), channel_id=1, source_target_pairs={{0,1},{1,2},{2,3},{3,4},{4,5},{5,6},{6,7},{7,8},{8,9},{9,10},{10,1... | collective-permute-start | bytes 1327112 | tf_op jit(solution)/shard_map/ppermute | solution.py:16
  2.4 6.9 %collective-permute-start.3 = (bf16[6,12,12,256]{3,2,1,0:T(8,128)(2,1)}, bf16[6,12,12,256]{3,2,1,0:T(8,128)(2,1)S(1)}, u32[]{:S(2)}, u32[]{:S(2)}) collective-permute-start(bf16[6,12,12,256]{3,2,1,0:T(8,128)(2,1)} %param.18), channel_id=1, source_target_pairs={{1,0},{2,1},{3,2},{4,3},{5,4},{6,5},{7,6},{8,7},{9,8},{10,9},{11,1... | collective-permute-start | bytes 1327112 | tf_op jit(solution)/shard_map/ppermute | solution.py:19
  29.9 6.7 %collective-permute-start = (bf16[12,12,256]{2,1,0:T(8,128)(2,1)}, bf16[12,12,256]{2,1,0:T(8,128)(2,1)S(1)}, u32[]{:S(2)}, u32[]{:S(2)}) collective-permute-start(bf16[12,12,256]{2,1,0:T(8,128)(2,1)} %fusion.397), channel_id=1, source_target_pairs={{0,64},{64,128},{128,192},{192,256},{256,320},{320,384},{384,448},... | collective-permute-start | bytes 221192 | tf_op jit(solution)/shard_map/while/body/eval_jaxpr/ppermute | solution.py:27
  45.5 6.7 %collective-permute-start = (bf16[12,12,256]{2,1,0:T(8,128)(2,1)}, bf16[12,12,256]{2,1,0:T(8,128)(2,1)S(1)}, u32[]{:S(2)}, u32[]{:S(2)}) collective-permute-start(bf16[12,12,256]{2,1,0:T(8,128)(2,1)} %fusion.397), channel_id=1, source_target_pairs={{0,64},{64,128},{128,192},{192,256},{256,320},{320,384},{384,448},... | collective-permute-start | bytes 221192 | tf_op jit(solution)/shard_map/while/body/eval_jaxpr/ppermute | solution.py:27
  61.1 6.7 %collective-permute-start = (bf16[12,12,256]{2,1,0:T(8,128)(2,1)}, bf16[12,12,256]{2,1,0:T(8,128)(2,1)S(1)}, u32[]{:S(2)}, u32[]{:S(2)}) collective-permute-start(bf16[12,12,256]{2,1,0:T(8,128)(2,1)} %fusion.397), channel_id=1, source_target_pairs={{0,64},{64,128},{128,192},{192,256},{256,320},{320,384},{384,448},... | collective-permute-start | bytes 221192 | tf_op jit(solution)/shard_map/while/body/eval_jaxpr/ppermute | solution.py:27
  76.8 6.7 %collective-permute-start = (bf16[12,12,256]{2,1,0:T(8,128)(2,1)}, bf16[12,12,256]{2,1,0:T(8,128)(2,1)S(1)}, u32[]{:S(2)}, u32[]{:S(2)}) collective-permute-start(bf16[12,12,256]{2,1,0:T(8,128)(2,1)} %fusion.397), channel_id=1, source_target_pairs={{0,64},{64,128},{128,192},{192,256},{256,320},{320,384},{384,448},... | collective-permute-start | bytes 221192 | tf_op jit(solution)/shard_map/while/body/eval_jaxpr/ppermute | solution.py:27
  92.4 7.0 %collective-permute-start = (bf16[12,12,256]{2,1,0:T(8,128)(2,1)}, bf16[12,12,256]{2,1,0:T(8,128)(2,1)S(1)}, u32[]{:S(2)}, u32[]{:S(2)}) collective-permute-start(bf16[12,12,256]{2,1,0:T(8,128)(2,1)} %fusion.397), channel_id=1, source_target_pairs={{0,64},{64,128},{128,192},{192,256},{256,320},{320,384},{384,448},... | collective-permute-start | bytes 221192 | tf_op jit(solution)/shard_map/while/body/eval_jaxpr/ppermute | solution.py:27
  108.3 7.3 %collective-permute-start = (bf16[12,12,256]{2,1,0:T(8,128)(2,1)}, bf16[12,12,256]{2,1,0:T(8,128)(2,1)S(1)}, u32[]{:S(2)}, u32[]{:S(2)}) collective-permute-start(bf16[12,12,256]{2,1,0:T(8,128)(2,1)} %fusion.397), channel_id=1, source_target_pairs={{0,64},{64,128},{128,192},{192,256},{256,320},{320,384},{384,448},... | collective-permute-start | bytes 221192 | tf_op jit(solution)/shard_map/while/body/eval_jaxpr/ppermute | solution.py:27
  124.6 7.6 %collective-permute-start = (bf16[12,12,256]{2,1,0:T(8,128)(2,1)}, bf16[12,12,256]{2,1,0:T(8,128)(2,1)S(1)}, u32[]{:S(2)}, u32[]{:S(2)}) collective-permute-start(bf16[12,12,256]{2,1,0:T(8,128)(2,1)} %fusion.397), channel_id=1, source_target_pairs={{0,64},{64,128},{128,192},{192,256},{256,320},{320,384},{384,448},... | collective-permute-start | bytes 221192 | tf_op jit(solution)/shard_map/while/body/eval_jaxpr/ppermute | solution.py:27
  141.1 8.2 %collective-permute-start = (bf16[12,12,256]{2,1,0:T(8,128)(2,1)}, bf16[12,12,256]{2,1,0:T(8,128)(2,1)S(1)}, u32[]{:S(2)}, u32[]{:S(2)}) collective-permute-start(bf16[12,12,256]{2,1,0:T(8,128)(2,1)} %fusion.397), channel_id=1, source_target_pairs={{0,64},{64,128},{128,192},{192,256},{256,320},{320,384},{384,448},... | collective-permute-start | bytes 221192 | tf_op jit(solution)/shard_map/while/body/eval_jaxpr/ppermute | solution.py:27
  158.2 7.3 %collective-permute-start = (bf16[12,12,256]{2,1,0:T(8,128)(2,1)}, bf16[12,12,256]{2,1,0:T(8,128)(2,1)S(1)}, u32[]{:S(2)}, u32[]{:S(2)}) collective-permute-start(bf16[12,12,256]{2,1,0:T(8,128)(2,1)} %fusion.397), channel_id=1, source_target_pairs={{0,64},{64,128},{128,192},{192,256},{256,320},{320,384},{384,448},... | collective-permute-start | bytes 221192 | tf_op jit(solution)/shard_map/while/body/eval_jaxpr/ppermute | solution.py:27
  170.8 6.4 %copy-start.3 = (f32[1,256]{1,0:T(1,128)S(1)}, f32[1,256]{1,0:T(1,128)}, u32[]{:S(2)}) copy-start(f32[1,256]{1,0:T(1,128)} %get-tuple-element.1769) | copy-start | bytes 3076 | tf_op jit(solution)/shard_map/while
  179.4 9.9 %collective-permute-start.1 = (bf16[12,12,256]{2,1,0:T(8,128)(2,1)S(1)}, bf16[12,12,256]{2,1,0:T(8,128)(2,1)S(1)}, u32[]{:S(2)}, u32[]{:S(2)}) collective-permute-start(bf16[12,12,256]{2,1,0:T(8,128)(2,1)S(1)} %fusion.415), channel_id=1, source_target_pairs={{64,0},{128,64},{192,128},{256,192},{320,256},{384,320},{448,384},... | collective-permute-start | bytes 221192 | tf_op jit(solution)/shard_map/while/body/eval_jaxpr/ppermute | solution.py:27
  195.1 6.4 %copy-start.3 = (f32[1,256]{1,0:T(1,128)S(1)}, f32[1,256]{1,0:T(1,128)}, u32[]{:S(2)}) copy-start(f32[1,256]{1,0:T(1,128)} %get-tuple-element.1769) | copy-start | bytes 3076 | tf_op jit(solution)/shard_map/while
  195.1 6.3 %copy-start.4 = (f32[1,256]{1,0:T(1,128)S(1)}, f32[1,256]{1,0:T(1,128)}, u32[]{:S(2)}) copy-start(f32[1,256]{1,0:T(1,128)} %get-tuple-element.1770) | copy-start | bytes 3076 | tf_op jit(solution)/shard_map/while
  195.1 6.3 %copy-start.5 = (f32[1,256]{1,0:T(1,128)S(1)}, f32[1,256]{1,0:T(1,128)}, u32[]{:S(2)}) copy-start(f32[1,256]{1,0:T(1,128)} %get-tuple-element.1771) | copy-start | bytes 3076 | tf_op jit(solution)/shard_map/while
  195.1 6.3 %copy-start.6 = (f32[1,256]{1,0:T(1,128)S(1)}, f32[1,256]{1,0:T(1,128)}, u32[]{:S(2)}) copy-start(f32[1,256]{1,0:T(1,128)} %get-tuple-element.1801) | copy-start | bytes 3076 | tf_op jit(solution)/shard_map/while
  195.1 6.3 %copy-start.7 = (f32[1,256]{1,0:T(1,128)S(1)}, f32[1,256]{1,0:T(1,128)}, u32[]{:S(2)}) copy-start(f32[1,256]{1,0:T(1,128)} %get-tuple-element.1772) | copy-start | bytes 3076 | tf_op jit(solution)/shard_map/while
  195.1 6.3 %copy-start.8 = (f32[1,256]{1,0:T(1,128)S(1)}, f32[1,256]{1,0:T(1,128)}, u32[]{:S(2)}) copy-start(f32[1,256]{1,0:T(1,128)} %get-tuple-element.1773) | copy-start | bytes 3076 | tf_op jit(solution)/shard_map/while
  195.1 6.3 %copy-start.9 = (f32[1,256]{1,0:T(1,128)S(1)}, f32[1,256]{1,0:T(1,128)}, u32[]{:S(2)}) copy-start(f32[1,256]{1,0:T(1,128)} %get-tuple-element.1774) | copy-start | bytes 3076 | tf_op jit(solution)/shard_map/while
  195.1 6.3 %copy-start.10 = (f32[1,256]{1,0:T(1,128)S(1)}, f32[1,256]{1,0:T(1,128)}, u32[]{:S(2)}) copy-start(f32[1,256]{1,0:T(1,128)} %get-tuple-element.1775) | copy-start | bytes 3076 | tf_op jit(solution)/shard_map/while
  195.2 6.3 %copy-start.11 = (f32[1,256]{1,0:T(1,128)S(1)}, f32[1,256]{1,0:T(1,128)}, u32[]{:S(2)}) copy-start(f32[1,256]{1,0:T(1,128)} %get-tuple-element.1776) | copy-start | bytes 3076 | tf_op jit(solution)/shard_map/while
  195.2 6.3 %copy-start.12 = (f32[1,256]{1,0:T(1,128)S(1)}, f32[1,256]{1,0:T(1,128)}, u32[]{:S(2)}) copy-start(f32[1,256]{1,0:T(1,128)} %get-tuple-element.1777) | copy-start | bytes 3076 | tf_op jit(solution)/shard_map/while
  195.2 6.3 %copy-start.13 = (f32[1,256]{1,0:T(1,128)S(1)}, f32[1,256]{1,0:T(1,128)}, u32[]{:S(2)}) copy-start(f32[1,256]{1,0:T(1,128)} %get-tuple-element.1778) | copy-start | bytes 3076 | tf_op jit(solution)/shard_map/while
  195.2 6.3 %copy-start.14 = (f32[1,256]{1,0:T(1,128)S(1)}, f32[1,256]{1,0:T(1,128)}, u32[]{:S(2)}) copy-start(f32[1,256]{1,0:T(1,128)} %get-tuple-element.1779) | copy-start | bytes 3076 | tf_op jit(solution)/shard_map/while
  195.2 6.3 %copy-start.15 = (f32[1,256]{1,0:T(1,128)S(1)}, f32[1,256]{1,0:T(1,128)}, u32[]{:S(2)}) copy-start(f32[1,256]{1,0:T(1,128)} %get-tuple-element.1780) | copy-start | bytes 3076 | tf_op jit(solution)/shard_map/while
  195.2 6.3 %copy-start.16 = (f32[1,256]{1,0:T(1,128)S(1)}, f32[1,256]{1,0:T(1,128)}, u32[]{:S(2)}) copy-start(f32[1,256]{1,0:T(1,128)} %get-tuple-element.1781) | copy-start | bytes 3076 | tf_op jit(solution)/shard_map/while
  203.6 9.9 %collective-permute-start.1 = (bf16[12,12,256]{2,1,0:T(8,128)(2,1)S(1)}, bf16[12,12,256]{2,1,0:T(8,128)(2,1)S(1)}, u32[]{:S(2)}, u32[]{:S(2)}) collective-permute-start(bf16[12,12,256]{2,1,0:T(8,128)(2,1)S(1)} %fusion.415), channel_id=1, source_target_pairs={{64,0},{128,64},{192,128},{256,192},{320,256},{384,320},{448,384},... | collective-permute-start | bytes 221192 | tf_op jit(solution)/shard_map/while/body/eval_jaxpr/ppermute | solution.py:27
  219.4 6.4 %copy-start.3 = (f32[1,256]{1,0:T(1,128)S(1)}, f32[1,256]{1,0:T(1,128)}, u32[]{:S(2)}) copy-start(f32[1,256]{1,0:T(1,128)} %get-tuple-element.1769) | copy-start | bytes 3076 | tf_op jit(solution)/shard_map/while
  228.0 9.9 %collective-permute-start.1 = (bf16[12,12,256]{2,1,0:T(8,128)(2,1)S(1)}, bf16[12,12,256]{2,1,0:T(8,128)(2,1)S(1)}, u32[]{:S(2)}, u32[]{:S(2)}) collective-permute-start(bf16[12,12,256]{2,1,0:T(8,128)(2,1)S(1)} %fusion.415), channel_id=1, source_target_pairs={{64,0},{128,64},{192,128},{256,192},{320,256},{384,320},{448,384},... | collective-permute-start | bytes 221192 | tf_op jit(solution)/shard_map/while/body/eval_jaxpr/ppermute | solution.py:27
  243.7 6.3 %copy-start.3 = (f32[1,256]{1,0:T(1,128)S(1)}, f32[1,256]{1,0:T(1,128)}, u32[]{:S(2)}) copy-start(f32[1,256]{1,0:T(1,128)} %get-tuple-element.1769) | copy-start | bytes 3076 | tf_op jit(solution)/shard_map/while
  252.3 7.0 %collective-permute-start.1 = (bf16[12,12,256]{2,1,0:T(8,128)(2,1)S(1)}, bf16[12,12,256]{2,1,0:T(8,128)(2,1)S(1)}, u32[]{:S(2)}, u32[]{:S(2)}) collective-permute-start(bf16[12,12,256]{2,1,0:T(8,128)(2,1)S(1)} %fusion.415), channel_id=1, source_target_pairs={{64,0},{128,64},{192,128},{256,192},{320,256},{384,320},{448,384},... | collective-permute-start | bytes 221192 | tf_op jit(solution)/shard_map/while/body/eval_jaxpr/ppermute | solution.py:27
  265.1 6.3 %copy-start.3 = (f32[1,256]{1,0:T(1,128)S(1)}, f32[1,256]{1,0:T(1,128)}, u32[]{:S(2)}) copy-start(f32[1,256]{1,0:T(1,128)} %get-tuple-element.1769) | copy-start | bytes 3076 | tf_op jit(solution)/shard_map/while
  273.7 7.2 %collective-permute-start.1 = (bf16[12,12,256]{2,1,0:T(8,128)(2,1)S(1)}, bf16[12,12,256]{2,1,0:T(8,128)(2,1)S(1)}, u32[]{:S(2)}, u32[]{:S(2)}) collective-permute-start(bf16[12,12,256]{2,1,0:T(8,128)(2,1)S(1)} %fusion.415), channel_id=1, source_target_pairs={{64,0},{128,64},{192,128},{256,192},{320,256},{384,320},{448,384},... | collective-permute-start | bytes 221192 | tf_op jit(solution)/shard_map/while/body/eval_jaxpr/ppermute | solution.py:27
  286.7 6.3 %copy-start.3 = (f32[1,256]{1,0:T(1,128)S(1)}, f32[1,256]{1,0:T(1,128)}, u32[]{:S(2)}) copy-start(f32[1,256]{1,0:T(1,128)} %get-tuple-element.1769) | copy-start | bytes 3076 | tf_op jit(solution)/shard_map/while
  295.3 7.2 %collective-permute-start.1 = (bf16[12,12,256]{2,1,0:T(8,128)(2,1)S(1)}, bf16[12,12,256]{2,1,0:T(8,128)(2,1)S(1)}, u32[]{:S(2)}, u32[]{:S(2)}) collective-permute-start(bf16[12,12,256]{2,1,0:T(8,128)(2,1)S(1)} %fusion.415), channel_id=1, source_target_pairs={{64,0},{128,64},{192,128},{256,192},{320,256},{384,320},{448,384},... | collective-permute-start | bytes 221192 | tf_op jit(solution)/shard_map/while/body/eval_jaxpr/ppermute | solution.py:27
  308.3 6.3 %copy-start.3 = (f32[1,256]{1,0:T(1,128)S(1)}, f32[1,256]{1,0:T(1,128)}, u32[]{:S(2)}) copy-start(f32[1,256]{1,0:T(1,128)} %get-tuple-element.1769) | copy-start | bytes 3076 | tf_op jit(solution)/shard_map/while
  316.9 7.2 %collective-permute-start.1 = (bf16[12,12,256]{2,1,0:T(8,128)(2,1)S(1)}, bf16[12,12,256]{2,1,0:T(8,128)(2,1)S(1)}, u32[]{:S(2)}, u32[]{:S(2)}) collective-permute-start(bf16[12,12,256]{2,1,0:T(8,128)(2,1)S(1)} %fusion.415), channel_id=1, source_target_pairs={{64,0},{128,64},{192,128},{256,192},{320,256},{384,320},{448,384},... | collective-permute-start | bytes 221192 | tf_op jit(solution)/shard_map/while/body/eval_jaxpr/ppermute | solution.py:27
  329.9 6.3 %copy-start.3 = (f32[1,256]{1,0:T(1,128)S(1)}, f32[1,256]{1,0:T(1,128)}, u32[]{:S(2)}) copy-start(f32[1,256]{1,0:T(1,128)} %get-tuple-element.1769) | copy-start | bytes 3076 | tf_op jit(solution)/shard_map/while
  338.4 7.2 %collective-permute-start.1 = (bf16[12,12,256]{2,1,0:T(8,128)(2,1)S(1)}, bf16[12,12,256]{2,1,0:T(8,128)(2,1)S(1)}, u32[]{:S(2)}, u32[]{:S(2)}) collective-permute-start(bf16[12,12,256]{2,1,0:T(8,128)(2,1)S(1)} %fusion.415), channel_id=1, source_target_pairs={{64,0},{128,64},{192,128},{256,192},{320,256},{384,320},{448,384},... | collective-permute-start | bytes 221192 | tf_op jit(solution)/shard_map/while/body/eval_jaxpr/ppermute | solution.py:27
  351.5 6.3 %copy-start.3 = (f32[1,256]{1,0:T(1,128)S(1)}, f32[1,256]{1,0:T(1,128)}, u32[]{:S(2)}) copy-start(f32[1,256]{1,0:T(1,128)} %get-tuple-element.1769) | copy-start | bytes 3076 | tf_op jit(solution)/shard_map/while
  360.0 7.2 %collective-permute-start.1 = (bf16[12,12,256]{2,1,0:T(8,128)(2,1)S(1)}, bf16[12,12,256]{2,1,0:T(8,128)(2,1)S(1)}, u32[]{:S(2)}, u32[]{:S(2)}) collective-permute-start(bf16[12,12,256]{2,1,0:T(8,128)(2,1)S(1)} %fusion.415), channel_id=1, source_target_pairs={{64,0},{128,64},{192,128},{256,192},{320,256},{384,320},{448,384},... | collective-permute-start | bytes 221192 | tf_op jit(solution)/shard_map/while/body/eval_jaxpr/ppermute | solution.py:27
  387.1 4.8 %collective-permute-start.4 = (f32[275200]{0:T(1024)S(1)}, f32[275200]{0:T(1024)}, u32[]{:S(2)}, u32[]{:S(2)}) collective-permute-start(f32[275200]{0:T(1024)S(1)} %pad_maximum_fusion.1), channel_id=1, source_target_pairs={{0,1},{1,0},{2,3},{3,2},{4,5},{5,4},{6,7},{7,6},{8,9},{9,8},{10,11... | collective-permute-start | bytes 3302408 | tf_op jit(solution)/shard_map/ppermute | solution.py:164
  396.8 21.4 %collective-permute-start.5 = (f32[144128]{0:T(1024)S(1)}, f32[144128]{0:T(1024)S(1)}, u32[]{:S(2)}, u32[]{:S(2)}) collective-permute-start(f32[144128]{0:T(1024)S(1)} %pad_maximum_fusion.2), channel_id=1, source_target_pairs={{0,2},{1,3},{2,0},{3,1},{4,6},{5,7},{6,4},{7,5},{8,10},{9,11},{10,... | collective-permute-start | bytes 1729544 | tf_op jit(solution)/shard_map/ppermute | solution.py:164
  419.2 11.6 %collective-permute-start.6 = (f32[78592]{0:T(1024)S(1)}, f32[78592]{0:T(1024)S(1)}, u32[]{:S(2)}, u32[]{:S(2)}) collective-permute-start(f32[78592]{0:T(1024)S(1)} %pad_maximum_fusion.3), channel_id=1, source_target_pairs={{0,16},{1,17},{2,18},{3,19},{4,20},{5,21},{6,22},{7,23},{8,24},{9,... | collective-permute-start | bytes 943112 | tf_op jit(solution)/shard_map/ppermute | solution.py:164
  431.4 11.8 %collective-permute-start.7 = (f32[45824]{0:T(1024)S(1)}, f32[45824]{0:T(1024)S(1)}, u32[]{:S(2)}, u32[]{:S(2)}) collective-permute-start(f32[45824]{0:T(1024)S(1)} %pad_maximum_fusion.4), channel_id=1, source_target_pairs={{0,4},{1,5},{2,6},{3,7},{4,0},{5,1},{6,2},{7,3},{8,12},{9,13},{10,... | collective-permute-start | bytes 549896 | tf_op jit(solution)/shard_map/ppermute | solution.py:164
  443.5 8.2 %collective-permute-start.8 = (f32[29440]{0:T(1024)S(1)}, f32[29440]{0:T(1024)S(1)}, u32[]{:S(2)}, u32[]{:S(2)}) collective-permute-start(f32[29440]{0:T(1024)S(1)} %pad_maximum_fusion.5), channel_id=1, source_target_pairs={{0,32},{1,33},{2,34},{3,35},{4,36},{5,37},{6,38},{7,39},{8,40},{9,... | collective-permute-start | bytes 353288 | tf_op jit(solution)/shard_map/ppermute | solution.py:164
  453.2 10.3 %collective-permute-start.9 = (f32[21248]{0:T(1024)S(1)}, f32[21248]{0:T(1024)S(1)}, u32[]{:S(2)}, u32[]{:S(2)}) collective-permute-start(f32[21248]{0:T(1024)S(1)} %pad_maximum_fusion.6), channel_id=1, source_target_pairs={{0,8},{1,9},{2,10},{3,11},{4,12},{5,13},{6,14},{7,15},{8,0},{9,1},... | collective-permute-start | bytes 254984 | tf_op jit(solution)/shard_map/ppermute | solution.py:164
  (205 other events, 1005.5 us)

commit v2 on v1

--- a/solution.py
+++ b/solution.py
@@ -102,7 +102,7 @@
     ) * (1.0 / math.sqrt(2.0 * math.pi))
     ct_mixed = (ct_hidden * slope).astype(jnp.bfloat16)
     g_in = jnp.dot(
-        normalized_input.reshape(-1, channels).T, ct_mixed, preferred_element_type=jnp.float32
+        ct_mixed.T, normalized_input.reshape(-1, channels), preferred_element_type=jnp.float32
     )
     normalized_cotangent = (
         jnp.dot(ct_mixed, proj_in.T, preferred_element_type=jnp.float32)
@@ -139,36 +139,30 @@
     return (ct_inputs.astype(jnp.bfloat16), (g_kernel, norm_gain_gradient, g_in, g_out, g_scale))
 
 
-def dp_reduce(g_in, g_out, small, axis):
+def dp_reduce(g_in_t, g_out, small, axis):
     holders = lax.axis_size(axis)
     bits = holders.bit_length() - 1
     assert 1 << bits == holders
     me = lax.axis_index(axis)
-    channels, hidden = g_in.shape
+    hidden, channels = g_out.shape
     share = hidden // holders
-    blocks_in = g_in.reshape(channels, holders, share).transpose(1, 0, 2).reshape(holders, -1)
-    blocks_out = g_out.reshape(holders, share * channels)
-    big = jnp.concatenate([blocks_in, blocks_out], axis=1)
-    width = big.shape[1]
-    big = big.reshape((2,) * bits + (width,))
+    big = jnp.stack([g_in_t, g_out]).reshape((2,) + (2,) * bits + (share * channels,))
     remaining = list(range(bits - 1, -1, -1))
     order = [0] + [b for b in (1, 4, 2, 5, 3) if b < bits] + [b for b in range(6, bits)]
     for bit in order:
-        position = remaining.index(bit)
+        position = remaining.index(bit) + 1
         mine = (me >> bit) & 1
         keep = lax.dynamic_index_in_dim(big, mine, position, keepdims=False)
         send = lax.dynamic_index_in_dim(big, 1 - mine, position, keepdims=False)
-        shape = keep.shape
-        packet = jnp.concatenate([send.reshape(-1), small])
+        small = small.astype(jnp.bfloat16).astype(jnp.float32)
+        packet = jnp.concatenate([send.reshape(-1), small]).astype(jnp.bfloat16)
         pairs = [(d, d ^ (1 << bit)) for d in range(holders)]
-        got = lax.ppermute(packet, axis, pairs)
-        big = keep + got[: keep.size].reshape(shape)
+        got = lax.ppermute(packet, axis, pairs).astype(jnp.float32)
+        big = keep + got[: keep.size].reshape(keep.shape)
         small = small + got[keep.size :]
-        remaining.pop(position)
-    big = big.reshape(width)
-    s_in = big[: channels * share].reshape(channels, share)
-    s_out = big[channels * share :].reshape(share, channels)
-    return s_in, s_out, small
+        remaining.pop(position - 1)
+    big = big.reshape(2, share, channels)
+    return big[0].T, big[1], small
 
 
 def per_device(images, dw_kernel, ln_gain, w_in, w_out, layer_scale, scene_grad, view_slot):
@@ -232,6 +226,7 @@
         return (back_x[0], back_p)
 
     start_totals = jax.tree.map(lambda member: jnp.zeros(member.shape, jnp.float32), params)
+    start_totals = start_totals[:2] + (start_totals[2].T,) + start_totals[3:]
 
     def backward_tick(tick, carry):
         incoming, totals = carry

time: 472 us -> 414 us (0.88)
  other arithmetic: 161 us -> 135 us
  local copies, waits for them, and re-layouts: 86.2 us -> 68.5 us
  matrix products: 75.4 us -> 67.8 us
    dynamic_update_slice x36, other arithmetic: 45.8 us -> 28.2 us  [forward_tick(): lax.dynamic_update_index_in_dim(buf, val, index, 0)]
    ppermute x6, waiting for transfers between devices: 37.8 us -> 21.9 us  [dp_reduce(): got = lax.ppermute(packet, axis, pairs).astype(jnp.float32)]
    ppermute x18, waiting for transfers between devices: 25.5 us -> 37.7 us  [from_behind(): return lax.ppermute(block, axis, route)]
    concatenate x3 -> x0, local copies, waits for them, and re-layouts: 10.8 us -> none  [dp_reduce(): big = jnp.concatenate([blocks_in, blocks_out], axis=1)]
    dot_general x9, matrix products: 12.2 us -> 2.89 us  [block_backward(): jnp.dot(ct_mixed, proj_in.T, preferred_element_type=jnp.float32)]
    another operation x2 -> x10, local copies, waits for them, and re-layouts: 1.77 us -> 9.92 us
    mul x9, local copies, waits for them, and re-layouts: 6.34 us -> 0.09 us  [block_backward(): inverse_deviation * (standardized_cotangent - jnp.mean(standardized_cotan...]
    convert_element_type x9, other arithmetic: 6.28 us -> 0.18 us  [block_backward(): ct_back = (incoming * scale).astype(jnp.bfloat16).reshape(-1, channels)]
where the time goes in v2:
time: 414 us; the launch traced here: 411 us
  other arithmetic  135 us (33%)
  starting transfers between devices  75.2 us (18%)
  local copies, waits for them, and re-layouts  68.5 us (17%)
  matrix products  67.8 us (16%)
  waiting for transfers between devices  59.6 us (14%)
    ppermute x18, starting transfers between devices, from_behind(): return lax.ppermute(block, axis, route)  40.7 us
    ppermute x18, waiting for transfers between devices, from_behind(): return lax.ppermute(block, axis, route)  37.7 us
    ppermute x6, starting transfers between devices, dp_reduce(): got = lax.ppermute(packet, axis, pairs).astype(jnp.float32)  31.4 us
    dot_general x9, matrix products, block_forward(): jnp.dot(normalized_input.reshape(-1, channels), proj_in, preferred_elemen...  29 us
    dynamic_update_slice x36, other arithmetic, forward_tick(): lax.dynamic_update_index_in_dim(buf, val, index, 0)  28.2 us
    ppermute x6, waiting for transfers between devices, dp_reduce(): got = lax.ppermute(packet, axis, pairs).astype(jnp.float32)  21.9 us
    squeeze x9, other arithmetic, backward_step(): return (back_x[0], back_p)  19.4 us
    reduce_sum x27, other arithmetic, block_backward(): kernel_rows.append(jnp.sum(depthwise_cotangent * window, axis=(0, 1, 2)))  19.1 us
  transfers between devices with their start and end apart: 26, of which 15 were waited for; matrix products, arithmetic and copies ran while one was open for 16% of the time, Pallas kernels for 0%

profile of v2, /device:TPU:448, one launch (start us, length us, event | category | flops | bytes accessed | tf_op | source)
XLA Modules:
  0.0 410.7 jit_solution(14088091742316242441)
XLA Ops:
  8.2 2.5 pad_maximum_fusion
  19.3 138.5 %while.55 = (s32[]{:T(128)}, bf16[12,12,256]{2,1,0:T(8,128)(2,1)S(1)}, bf16[3,12,12,256]{3,2,1,0:T(8,128)(2,1)}, f32[3,1,12,12,256]{4,3,2,1,0:T(8,128)}, f32[3,1...) while((s32[]{:T(128)}, ...), condition=%wide.region_3.4_spmd, body=%wide.region_0.3_spmd.sunk | while | flops 164782528 | bytes 9613381 | solution.py:220
  23.3 3.2 bitcast_dynamic-update-slice_fusion.14
  30.5 3.7 collective-permute-done
  38.2 3.2 bitcast_dynamic-update-slice_fusion.14
  45.4 3.7 collective-permute-done
  53.1 3.2 bitcast_dynamic-update-slice_fusion.14
  60.3 3.7 collective-permute-done
  68.0 3.2 bitcast_dynamic-update-slice_fusion.14
  75.2 3.7 collective-permute-done
  82.9 3.2 bitcast_dynamic-update-slice_fusion.14
  90.1 3.7 collective-permute-done
  97.8 3.2 bitcast_dynamic-update-slice_fusion.14
  105.0 3.9 collective-permute-done
  112.9 3.2 bitcast_dynamic-update-slice_fusion.14
  120.1 4.5 %collective-permute-done = bf16[12,12,256]{2,1,0:T(8,128)(2,1)S(1)} collective-permute-done((bf16[12,12,256]{2,1,0:T(8,128)(2,1)}, bf16[12,12,256]{2,1,0:T(8,128)(2,1)S(1)}, u32[]{:S(2)}, u32[]{:S(2)}) %collective-permute-start) | collective-permute-done | bytes 73760 | tf_op jit(solution)/shard_map/while/body/eval_jaxpr/ppermute | solution.py:27
  128.6 3.2 bitcast_dynamic-update-slice_fusion.14
  135.8 5.8 %collective-permute-done = bf16[12,12,256]{2,1,0:T(8,128)(2,1)S(1)} collective-permute-done((bf16[12,12,256]{2,1,0:T(8,128)(2,1)}, bf16[12,12,256]{2,1,0:T(8,128)(2,1)S(1)}, u32[]{:S(2)}, u32[]{:S(2)}) %collective-permute-start) | collective-permute-done | bytes 73760 | tf_op jit(solution)/shard_map/while/body/eval_jaxpr/ppermute | solution.py:27
  145.6 3.2 bitcast_dynamic-update-slice_fusion.14
  152.8 5.0 %collective-permute-done = bf16[12,12,256]{2,1,0:T(8,128)(2,1)S(1)} collective-permute-done((bf16[12,12,256]{2,1,0:T(8,128)(2,1)}, bf16[12,12,256]{2,1,0:T(8,128)(2,1)S(1)}, u32[]{:S(2)}, u32[]{:S(2)}) %collective-permute-start) | collective-permute-done | bytes 73760 | tf_op jit(solution)/shard_map/while/body/eval_jaxpr/ppermute | solution.py:27
  158.4 178.5 %while.56 = (s32[]{:T(128)}, bf16[12,12,256]{2,1,0:T(8,128)(2,1)}, f32[49,256]{1,0:T(8,128)}, f32[256]{0:T(256)}, f32[1024,256]{1,0:T(8,128)S(1)}, /*index=5*/f3...) while((s32[]{:T(128)}, bf16[12,12,256]{2,1,0:T(8,128)(2,1)}, ...), condition=%wide.region_58.59_spmd.clone, body=%wide.region_4.58_spmd.clone.sunk | while | flops 313505280 | bytes 15141404 | solution.py:249
  167.2 2.2 fusion.420
  169.4 5.3 %collective-permute-start.1 = (bf16[12,12,256]{2,1,0:T(8,128)(2,1)S(1)}, bf16[12,12,256]{2,1,0:T(8,128)(2,1)}, u32[]{:S(2)}, u32[]{:S(2)}) collective-permute-start(bf16[12,12,256]{2,1,0:T(8,128)(2,1)S(1)} %fusion.420), channel_id=1, source_target_pairs={{64,0},{128,64},{192,128},{256,192},{320,256},{384,320},{448,384},... | collective-permute-start | bytes 221192 | tf_op jit(solution)/shard_map/while/body/eval_jaxpr/ppermute | solution.py:27
  189.1 2.2 fusion.420
  191.2 5.1 %collective-permute-start.1 = (bf16[12,12,256]{2,1,0:T(8,128)(2,1)S(1)}, bf16[12,12,256]{2,1,0:T(8,128)(2,1)}, u32[]{:S(2)}, u32[]{:S(2)}) collective-permute-start(bf16[12,12,256]{2,1,0:T(8,128)(2,1)S(1)} %fusion.420), channel_id=1, source_target_pairs={{64,0},{128,64},{192,128},{256,192},{320,256},{384,320},{448,384},... | collective-permute-start | bytes 221192 | tf_op jit(solution)/shard_map/while/body/eval_jaxpr/ppermute | solution.py:27
  210.8 2.2 fusion.420
  213.0 5.2 %collective-permute-start.1 = (bf16[12,12,256]{2,1,0:T(8,128)(2,1)S(1)}, bf16[12,12,256]{2,1,0:T(8,128)(2,1)}, u32[]{:S(2)}, u32[]{:S(2)}) collective-permute-start(bf16[12,12,256]{2,1,0:T(8,128)(2,1)S(1)} %fusion.420), channel_id=1, source_target_pairs={{64,0},{128,64},{192,128},{256,192},{320,256},{384,320},{448,384},... | collective-permute-start | bytes 221192 | tf_op jit(solution)/shard_map/while/body/eval_jaxpr/ppermute | solution.py:27
  232.6 2.2 fusion.420
  251.2 2.2 fusion.420
  253.3 2.3 collective-permute-start.1
  270.1 2.2 fusion.420
  272.2 2.3 collective-permute-start.1
  289.0 2.2 fusion.420
  291.1 2.3 collective-permute-start.1
  307.9 2.2 fusion.420
  310.1 2.3 collective-permute-start.1
  329.0 2.3 collective-permute-start.1
  338.6 3.1 copy_dynamic-update-slice_fusion.1
  354.6 9.2 %collective-permute-start.5 = (bf16[144128]{0:T(1024)(128)(2,1)S(1)}, bf16[144128]{0:T(1024)(128)(2,1)S(1)}, u32[]{:S(2)}, u32[]{:S(2)}) collective-permute-start(bf16[144128]{0:T(1024)(128)(2,1)S(1)} %pad_maximum_fusion.2), channel_id=1, source_target_pairs={{0,2},{1,3},{2,0},{3,1},{4,6},{5,7},{6,4},{7,5},{8,10},{9,11},{10,... | collective-permute-start | bytes 864776 | tf_op jit(solution)/shard_map/ppermute | solution.py:160
  364.4 6.6 %collective-permute-done.5 = bf16[144128]{0:T(1024)(128)(2,1)S(1)} collective-permute-done((bf16[144128]{0:T(1024)(128)(2,1)S(1)}, bf16[144128]{0:T(1024)(128)(2,1)S(1)}, u32[]{:S(2)}, u32[]{:S(2)}) %collective-permute-start.5) | collective-permute-done | bytes 288288 | tf_op jit(solution)/shard_map/ppermute | solution.py:160
  372.1 4.7 %collective-permute-start.6 = (bf16[78592]{0:T(1024)(128)(2,1)S(1)}, bf16[78592]{0:T(1024)(128)(2,1)S(1)}, u32[]{:S(2)}, u32[]{:S(2)}) collective-permute-start(bf16[78592]{0:T(1024)(128)(2,1)S(1)} %pad_maximum_fusion.3), channel_id=1, source_target_pairs={{0,16},{1,17},{2,18},{3,19},{4,20},{5,21},{6,22},{7,23},{8,24},{9,... | collective-permute-start | bytes 471560 | tf_op jit(solution)/shard_map/ppermute | solution.py:160
  376.8 3.5 collective-permute-done.6
  381.1 3.6 collective-permute-start.7
  384.9 4.6 %collective-permute-done.7 = bf16[45824]{0:T(1024)(128)(2,1)S(1)} collective-permute-done((bf16[45824]{0:T(1024)(128)(2,1)S(1)}, bf16[45824]{0:T(1024)(128)(2,1)S(1)}, u32[]{:S(2)}, u32[]{:S(2)}) %collective-permute-start.7) | collective-permute-done | bytes 91680 | tf_op jit(solution)/shard_map/ppermute | solution.py:160
  389.8 5.0 %collective-permute-start.8 = (bf16[29440]{0:T(1024)(128)(2,1)S(1)}, bf16[29440]{0:T(1024)(128)(2,1)S(1)}, u32[]{:S(2)}, u32[]{:S(2)}) collective-permute-start(bf16[29440]{0:T(1024)(128)(2,1)S(1)} %pad_maximum_fusion.5), channel_id=1, source_target_pairs={{0,32},{1,33},{2,34},{3,35},{4,36},{5,37},{6,38},{7,39},{8,40},{9,... | collective-permute-start | bytes 176648 | tf_op jit(solution)/shard_map/ppermute | solution.py:160
  394.8 2.6 collective-permute-done.8
  397.7 7.0 %collective-permute-start.9 = (bf16[21248]{0:T(1024)(128)(2,1)S(1)}, bf16[21248]{0:T(1024)(128)(2,1)S(1)}, u32[]{:S(2)}, u32[]{:S(2)}) collective-permute-start(bf16[21248]{0:T(1024)(128)(2,1)S(1)} %pad_maximum_fusion.6), channel_id=1, source_target_pairs={{0,8},{1,9},{2,10},{3,11},{4,12},{5,13},{6,14},{7,15},{8,0},{9,1},... | collective-permute-start | bytes 127496 | tf_op jit(solution)/shard_map/ppermute | solution.py:160
  404.7 2.8 collective-permute-done.9
  (777 shorter events, 239.7 us)
Async XLA Ops:
  0.6 7.6 %collective-permute-start.2 = (bf16[6,12,12,256]{3,2,1,0:T(8,128)(2,1)}, bf16[6,12,12,256]{3,2,1,0:T(8,128)(2,1)S(1)}, u32[]{:S(2)}, u32[]{:S(2)}) collective-permute-start(bf16[6,12,12,256]{3,2,1,0:T(8,128)(2,1)} %param.18), channel_id=1, source_target_pairs={{0,1},{1,2},{2,3},{3,4},{4,5},{5,6},{6,7},{7,8},{8,9},{9,10},{10,1... | collective-permute-start | bytes 1327112 | tf_op jit(solution)/shard_map/ppermute | solution.py:16
  2.4 5.8 %collective-permute-start.3 = (bf16[6,12,12,256]{3,2,1,0:T(8,128)(2,1)}, bf16[6,12,12,256]{3,2,1,0:T(8,128)(2,1)S(1)}, u32[]{:S(2)}, u32[]{:S(2)}) collective-permute-start(bf16[6,12,12,256]{3,2,1,0:T(8,128)(2,1)} %param.18), channel_id=1, source_target_pairs={{1,0},{2,1},{3,2},{4,3},{5,4},{6,5},{7,6},{8,7},{9,8},{10,9},{11,1... | collective-permute-start | bytes 1327112 | tf_op jit(solution)/shard_map/ppermute | solution.py:19
  27.5 6.7 %collective-permute-start = (bf16[12,12,256]{2,1,0:T(8,128)(2,1)}, bf16[12,12,256]{2,1,0:T(8,128)(2,1)S(1)}, u32[]{:S(2)}, u32[]{:S(2)}) collective-permute-start(bf16[12,12,256]{2,1,0:T(8,128)(2,1)} %fusion.402), channel_id=1, source_target_pairs={{0,64},{64,128},{128,192},{192,256},{256,320},{320,384},{384,448},... | collective-permute-start | bytes 221192 | tf_op jit(solution)/shard_map/while/body/eval_jaxpr/ppermute | solution.py:27
  42.4 6.7 %collective-permute-start = (bf16[12,12,256]{2,1,0:T(8,128)(2,1)}, bf16[12,12,256]{2,1,0:T(8,128)(2,1)S(1)}, u32[]{:S(2)}, u32[]{:S(2)}) collective-permute-start(bf16[12,12,256]{2,1,0:T(8,128)(2,1)} %fusion.402), channel_id=1, source_target_pairs={{0,64},{64,128},{128,192},{192,256},{256,320},{320,384},{384,448},... | collective-permute-start | bytes 221192 | tf_op jit(solution)/shard_map/while/body/eval_jaxpr/ppermute | solution.py:27
  57.3 6.7 %collective-permute-start = (bf16[12,12,256]{2,1,0:T(8,128)(2,1)}, bf16[12,12,256]{2,1,0:T(8,128)(2,1)S(1)}, u32[]{:S(2)}, u32[]{:S(2)}) collective-permute-start(bf16[12,12,256]{2,1,0:T(8,128)(2,1)} %fusion.402), channel_id=1, source_target_pairs={{0,64},{64,128},{128,192},{192,256},{256,320},{320,384},{384,448},... | collective-permute-start | bytes 221192 | tf_op jit(solution)/shard_map/while/body/eval_jaxpr/ppermute | solution.py:27
  72.1 6.7 %collective-permute-start = (bf16[12,12,256]{2,1,0:T(8,128)(2,1)}, bf16[12,12,256]{2,1,0:T(8,128)(2,1)S(1)}, u32[]{:S(2)}, u32[]{:S(2)}) collective-permute-start(bf16[12,12,256]{2,1,0:T(8,128)(2,1)} %fusion.402), channel_id=1, source_target_pairs={{0,64},{64,128},{128,192},{192,256},{256,320},{320,384},{384,448},... | collective-permute-start | bytes 221192 | tf_op jit(solution)/shard_map/while/body/eval_jaxpr/ppermute | solution.py:27
  87.0 6.7 %collective-permute-start = (bf16[12,12,256]{2,1,0:T(8,128)(2,1)}, bf16[12,12,256]{2,1,0:T(8,128)(2,1)S(1)}, u32[]{:S(2)}, u32[]{:S(2)}) collective-permute-start(bf16[12,12,256]{2,1,0:T(8,128)(2,1)} %fusion.402), channel_id=1, source_target_pairs={{0,64},{64,128},{128,192},{192,256},{256,320},{320,384},{384,448},... | collective-permute-start | bytes 221192 | tf_op jit(solution)/shard_map/while/body/eval_jaxpr/ppermute | solution.py:27
  101.9 6.9 %collective-permute-start = (bf16[12,12,256]{2,1,0:T(8,128)(2,1)}, bf16[12,12,256]{2,1,0:T(8,128)(2,1)S(1)}, u32[]{:S(2)}, u32[]{:S(2)}) collective-permute-start(bf16[12,12,256]{2,1,0:T(8,128)(2,1)} %fusion.402), channel_id=1, source_target_pairs={{0,64},{64,128},{128,192},{192,256},{256,320},{320,384},{384,448},... | collective-permute-start | bytes 221192 | tf_op jit(solution)/shard_map/while/body/eval_jaxpr/ppermute | solution.py:27
  117.1 7.5 %collective-permute-start = (bf16[12,12,256]{2,1,0:T(8,128)(2,1)}, bf16[12,12,256]{2,1,0:T(8,128)(2,1)S(1)}, u32[]{:S(2)}, u32[]{:S(2)}) collective-permute-start(bf16[12,12,256]{2,1,0:T(8,128)(2,1)} %fusion.402), channel_id=1, source_target_pairs={{0,64},{64,128},{128,192},{192,256},{256,320},{320,384},{384,448},... | collective-permute-start | bytes 221192 | tf_op jit(solution)/shard_map/while/body/eval_jaxpr/ppermute | solution.py:27
  132.8 8.8 %collective-permute-start = (bf16[12,12,256]{2,1,0:T(8,128)(2,1)}, bf16[12,12,256]{2,1,0:T(8,128)(2,1)S(1)}, u32[]{:S(2)}, u32[]{:S(2)}) collective-permute-start(bf16[12,12,256]{2,1,0:T(8,128)(2,1)} %fusion.402), channel_id=1, source_target_pairs={{0,64},{64,128},{128,192},{192,256},{256,320},{320,384},{384,448},... | collective-permute-start | bytes 221192 | tf_op jit(solution)/shard_map/while/body/eval_jaxpr/ppermute | solution.py:27
  149.8 8.0 %collective-permute-start = (bf16[12,12,256]{2,1,0:T(8,128)(2,1)}, bf16[12,12,256]{2,1,0:T(8,128)(2,1)S(1)}, u32[]{:S(2)}, u32[]{:S(2)}) collective-permute-start(bf16[12,12,256]{2,1,0:T(8,128)(2,1)} %fusion.402), channel_id=1, source_target_pairs={{0,64},{64,128},{128,192},{192,256},{256,320},{320,384},{384,448},... | collective-permute-start | bytes 221192 | tf_op jit(solution)/shard_map/while/body/eval_jaxpr/ppermute | solution.py:27
  158.4 8.2 %copy-start.7 = (f32[3,1,12,12,1]{3,2,4,1,0:T(8,128)}, f32[3,1,12,12,1]{3,2,4,1,0:T(8,128)S(1)}, u32[]{:S(2)}) copy-start(f32[3,1,12,12,1]{3,2,4,1,0:T(8,128)S(1)} %get-tuple-element.1962) | copy-start | bytes 5188 | tf_op jit(solution)/shard_map/while
  165.7 11.7 %copy-start.4 = (f32[49,256]{1,0:T(8,128)S(1)}, f32[49,256]{1,0:T(8,128)}, u32[]{:S(2)}) copy-start(f32[49,256]{1,0:T(8,128)} %get-tuple-element.1929) | copy-start | bytes 150532 | tf_op jit(solution)/shard_map/while
  169.4 10.3 %collective-permute-start.1 = (bf16[12,12,256]{2,1,0:T(8,128)(2,1)S(1)}, bf16[12,12,256]{2,1,0:T(8,128)(2,1)}, u32[]{:S(2)}, u32[]{:S(2)}) collective-permute-start(bf16[12,12,256]{2,1,0:T(8,128)(2,1)S(1)} %fusion.420), channel_id=1, source_target_pairs={{64,0},{128,64},{192,128},{256,192},{320,256},{384,320},{448,384},... | collective-permute-start | bytes 221192 | tf_op jit(solution)/shard_map/while/body/eval_jaxpr/ppermute | solution.py:27
  180.3 5.5 %copy-start.2 = (f32[49,256]{1,0:T(8,128)}, f32[49,256]{1,0:T(8,128)S(1)}, u32[]{:S(2)}) copy-start(f32[49,256]{1,0:T(8,128)S(1)} %get-tuple-element.1969) | copy-start | bytes 150532 | tf_op jit(solution)/shard_map/while
  180.3 8.3 %copy-start.7 = (f32[3,1,12,12,1]{3,2,4,1,0:T(8,128)}, f32[3,1,12,12,1]{3,2,4,1,0:T(8,128)S(1)}, u32[]{:S(2)}) copy-start(f32[3,1,12,12,1]{3,2,4,1,0:T(8,128)S(1)} %get-tuple-element.1962) | copy-start | bytes 5188 | tf_op jit(solution)/shard_map/while
  187.5 11.6 %copy-start.4 = (f32[49,256]{1,0:T(8,128)S(1)}, f32[49,256]{1,0:T(8,128)}, u32[]{:S(2)}) copy-start(f32[49,256]{1,0:T(8,128)} %get-tuple-element.1929) | copy-start | bytes 150532 | tf_op jit(solution)/shard_map/while
  191.2 10.2 %collective-permute-start.1 = (bf16[12,12,256]{2,1,0:T(8,128)(2,1)S(1)}, bf16[12,12,256]{2,1,0:T(8,128)(2,1)}, u32[]{:S(2)}, u32[]{:S(2)}) collective-permute-start(bf16[12,12,256]{2,1,0:T(8,128)(2,1)S(1)} %fusion.420), channel_id=1, source_target_pairs={{64,0},{128,64},{192,128},{256,192},{320,256},{384,320},{448,384},... | collective-permute-start | bytes 221192 | tf_op jit(solution)/shard_map/while/body/eval_jaxpr/ppermute | solution.py:27
  202.0 5.5 %copy-start.2 = (f32[49,256]{1,0:T(8,128)}, f32[49,256]{1,0:T(8,128)S(1)}, u32[]{:S(2)}) copy-start(f32[49,256]{1,0:T(8,128)S(1)} %get-tuple-element.1969) | copy-start | bytes 150532 | tf_op jit(solution)/shard_map/while
  202.0 8.3 %copy-start.7 = (f32[3,1,12,12,1]{3,2,4,1,0:T(8,128)}, f32[3,1,12,12,1]{3,2,4,1,0:T(8,128)S(1)}, u32[]{:S(2)}) copy-start(f32[3,1,12,12,1]{3,2,4,1,0:T(8,128)S(1)} %get-tuple-element.1962) | copy-start | bytes 5188 | tf_op jit(solution)/shard_map/while
  209.2 11.6 %copy-start.4 = (f32[49,256]{1,0:T(8,128)S(1)}, f32[49,256]{1,0:T(8,128)}, u32[]{:S(2)}) copy-start(f32[49,256]{1,0:T(8,128)} %get-tuple-element.1929) | copy-start | bytes 150532 | tf_op jit(solution)/shard_map/while
  213.0 10.2 %collective-permute-start.1 = (bf16[12,12,256]{2,1,0:T(8,128)(2,1)S(1)}, bf16[12,12,256]{2,1,0:T(8,128)(2,1)}, u32[]{:S(2)}, u32[]{:S(2)}) collective-permute-start(bf16[12,12,256]{2,1,0:T(8,128)(2,1)S(1)} %fusion.420), channel_id=1, source_target_pairs={{64,0},{128,64},{192,128},{256,192},{320,256},{384,320},{448,384},... | collective-permute-start | bytes 221192 | tf_op jit(solution)/shard_map/while/body/eval_jaxpr/ppermute | solution.py:27
  223.8 5.5 %copy-start.2 = (f32[49,256]{1,0:T(8,128)}, f32[49,256]{1,0:T(8,128)S(1)}, u32[]{:S(2)}) copy-start(f32[49,256]{1,0:T(8,128)S(1)} %get-tuple-element.1969) | copy-start | bytes 150532 | tf_op jit(solution)/shard_map/while
  223.8 8.3 %copy-start.7 = (f32[3,1,12,12,1]{3,2,4,1,0:T(8,128)}, f32[3,1,12,12,1]{3,2,4,1,0:T(8,128)S(1)}, u32[]{:S(2)}) copy-start(f32[3,1,12,12,1]{3,2,4,1,0:T(8,128)S(1)} %get-tuple-element.1962) | copy-start | bytes 5188 | tf_op jit(solution)/shard_map/while
  231.0 8.4 %copy-start.4 = (f32[49,256]{1,0:T(8,128)S(1)}, f32[49,256]{1,0:T(8,128)}, u32[]{:S(2)}) copy-start(f32[49,256]{1,0:T(8,128)} %get-tuple-element.1929) | copy-start | bytes 150532 | tf_op jit(solution)/shard_map/while
  234.8 7.0 %collective-permute-start.1 = (bf16[12,12,256]{2,1,0:T(8,128)(2,1)S(1)}, bf16[12,12,256]{2,1,0:T(8,128)(2,1)}, u32[]{:S(2)}, u32[]{:S(2)}) collective-permute-start(bf16[12,12,256]{2,1,0:T(8,128)(2,1)S(1)} %fusion.420), channel_id=1, source_target_pairs={{64,0},{128,64},{192,128},{256,192},{320,256},{384,320},{448,384},... | collective-permute-start | bytes 221192 | tf_op jit(solution)/shard_map/while/body/eval_jaxpr/ppermute | solution.py:27
  242.3 5.5 %copy-start.2 = (f32[49,256]{1,0:T(8,128)}, f32[49,256]{1,0:T(8,128)S(1)}, u32[]{:S(2)}) copy-start(f32[49,256]{1,0:T(8,128)S(1)} %get-tuple-element.1969) | copy-start | bytes 150532 | tf_op jit(solution)/shard_map/while
  242.4 8.3 %copy-start.7 = (f32[3,1,12,12,1]{3,2,4,1,0:T(8,128)}, f32[3,1,12,12,1]{3,2,4,1,0:T(8,128)S(1)}, u32[]{:S(2)}) copy-start(f32[3,1,12,12,1]{3,2,4,1,0:T(8,128)S(1)} %get-tuple-element.1962) | copy-start | bytes 5188 | tf_op jit(solution)/shard_map/while
  249.6 8.8 %copy-start.4 = (f32[49,256]{1,0:T(8,128)S(1)}, f32[49,256]{1,0:T(8,128)}, u32[]{:S(2)}) copy-start(f32[49,256]{1,0:T(8,128)} %get-tuple-element.1929) | copy-start | bytes 150532 | tf_op jit(solution)/shard_map/while
  253.3 7.4 %collective-permute-start.1 = (bf16[12,12,256]{2,1,0:T(8,128)(2,1)S(1)}, bf16[12,12,256]{2,1,0:T(8,128)(2,1)}, u32[]{:S(2)}, u32[]{:S(2)}) collective-permute-start(bf16[12,12,256]{2,1,0:T(8,128)(2,1)S(1)} %fusion.420), channel_id=1, source_target_pairs={{64,0},{128,64},{192,128},{256,192},{320,256},{384,320},{448,384},... | collective-permute-start | bytes 221192 | tf_op jit(solution)/shard_map/while/body/eval_jaxpr/ppermute | solution.py:27
  261.3 8.3 %copy-start.7 = (f32[3,1,12,12,1]{3,2,4,1,0:T(8,128)}, f32[3,1,12,12,1]{3,2,4,1,0:T(8,128)S(1)}, u32[]{:S(2)}) copy-start(f32[3,1,12,12,1]{3,2,4,1,0:T(8,128)S(1)} %get-tuple-element.1962) | copy-start | bytes 5188 | tf_op jit(solution)/shard_map/while
  268.5 8.8 %copy-start.4 = (f32[49,256]{1,0:T(8,128)S(1)}, f32[49,256]{1,0:T(8,128)}, u32[]{:S(2)}) copy-start(f32[49,256]{1,0:T(8,128)} %get-tuple-element.1929) | copy-start | bytes 150532 | tf_op jit(solution)/shard_map/while
  272.2 7.4 %collective-permute-start.1 = (bf16[12,12,256]{2,1,0:T(8,128)(2,1)S(1)}, bf16[12,12,256]{2,1,0:T(8,128)(2,1)}, u32[]{:S(2)}, u32[]{:S(2)}) collective-permute-start(bf16[12,12,256]{2,1,0:T(8,128)(2,1)S(1)} %fusion.420), channel_id=1, source_target_pairs={{64,0},{128,64},{192,128},{256,192},{320,256},{384,320},{448,384},... | collective-permute-start | bytes 221192 | tf_op jit(solution)/shard_map/while/body/eval_jaxpr/ppermute | solution.py:27
  280.2 8.3 %copy-start.7 = (f32[3,1,12,12,1]{3,2,4,1,0:T(8,128)}, f32[3,1,12,12,1]{3,2,4,1,0:T(8,128)S(1)}, u32[]{:S(2)}) copy-start(f32[3,1,12,12,1]{3,2,4,1,0:T(8,128)S(1)} %get-tuple-element.1962) | copy-start | bytes 5188 | tf_op jit(solution)/shard_map/while
  287.4 8.8 %copy-start.4 = (f32[49,256]{1,0:T(8,128)S(1)}, f32[49,256]{1,0:T(8,128)}, u32[]{:S(2)}) copy-start(f32[49,256]{1,0:T(8,128)} %get-tuple-element.1929) | copy-start | bytes 150532 | tf_op jit(solution)/shard_map/while
  291.1 7.4 %collective-permute-start.1 = (bf16[12,12,256]{2,1,0:T(8,128)(2,1)S(1)}, bf16[12,12,256]{2,1,0:T(8,128)(2,1)}, u32[]{:S(2)}, u32[]{:S(2)}) collective-permute-start(bf16[12,12,256]{2,1,0:T(8,128)(2,1)S(1)} %fusion.420), channel_id=1, source_target_pairs={{64,0},{128,64},{192,128},{256,192},{320,256},{384,320},{448,384},... | collective-permute-start | bytes 221192 | tf_op jit(solution)/shard_map/while/body/eval_jaxpr/ppermute | solution.py:27
  299.1 8.3 %copy-start.7 = (f32[3,1,12,12,1]{3,2,4,1,0:T(8,128)}, f32[3,1,12,12,1]{3,2,4,1,0:T(8,128)S(1)}, u32[]{:S(2)}) copy-start(f32[3,1,12,12,1]{3,2,4,1,0:T(8,128)S(1)} %get-tuple-element.1962) | copy-start | bytes 5188 | tf_op jit(solution)/shard_map/while
  306.3 8.8 %copy-start.4 = (f32[49,256]{1,0:T(8,128)S(1)}, f32[49,256]{1,0:T(8,128)}, u32[]{:S(2)}) copy-start(f32[49,256]{1,0:T(8,128)} %get-tuple-element.1929) | copy-start | bytes 150532 | tf_op jit(solution)/shard_map/while
  310.1 7.4 %collective-permute-start.1 = (bf16[12,12,256]{2,1,0:T(8,128)(2,1)S(1)}, bf16[12,12,256]{2,1,0:T(8,128)(2,1)}, u32[]{:S(2)}, u32[]{:S(2)}) collective-permute-start(bf16[12,12,256]{2,1,0:T(8,128)(2,1)S(1)} %fusion.420), channel_id=1, source_target_pairs={{64,0},{128,64},{192,128},{256,192},{320,256},{384,320},{448,384},... | collective-permute-start | bytes 221192 | tf_op jit(solution)/shard_map/while/body/eval_jaxpr/ppermute | solution.py:27
  318.0 8.3 %copy-start.7 = (f32[3,1,12,12,1]{3,2,4,1,0:T(8,128)}, f32[3,1,12,12,1]{3,2,4,1,0:T(8,128)S(1)}, u32[]{:S(2)}) copy-start(f32[3,1,12,12,1]{3,2,4,1,0:T(8,128)S(1)} %get-tuple-element.1962) | copy-start | bytes 5188 | tf_op jit(solution)/shard_map/while
  325.2 8.8 %copy-start.4 = (f32[49,256]{1,0:T(8,128)S(1)}, f32[49,256]{1,0:T(8,128)}, u32[]{:S(2)}) copy-start(f32[49,256]{1,0:T(8,128)} %get-tuple-element.1929) | copy-start | bytes 150532 | tf_op jit(solution)/shard_map/while
  329.0 7.4 %collective-permute-start.1 = (bf16[12,12,256]{2,1,0:T(8,128)(2,1)S(1)}, bf16[12,12,256]{2,1,0:T(8,128)(2,1)}, u32[]{:S(2)}, u32[]{:S(2)}) collective-permute-start(bf16[12,12,256]{2,1,0:T(8,128)(2,1)S(1)} %fusion.420), channel_id=1, source_target_pairs={{64,0},{128,64},{192,128},{256,192},{320,256},{384,320},{448,384},... | collective-permute-start | bytes 221192 | tf_op jit(solution)/shard_map/while/body/eval_jaxpr/ppermute | solution.py:27
  346.1 3.8 collective-permute-start.4
  354.6 16.3 %collective-permute-start.5 = (bf16[144128]{0:T(1024)(128)(2,1)S(1)}, bf16[144128]{0:T(1024)(128)(2,1)S(1)}, u32[]{:S(2)}, u32[]{:S(2)}) collective-permute-start(bf16[144128]{0:T(1024)(128)(2,1)S(1)} %pad_maximum_fusion.2), channel_id=1, source_target_pairs={{0,2},{1,3},{2,0},{3,1},{4,6},{5,7},{6,4},{7,5},{8,10},{9,11},{10,... | collective-permute-start | bytes 864776 | tf_op jit(solution)/shard_map/ppermute | solution.py:160
  372.1 8.2 %collective-permute-start.6 = (bf16[78592]{0:T(1024)(128)(2,1)S(1)}, bf16[78592]{0:T(1024)(128)(2,1)S(1)}, u32[]{:S(2)}, u32[]{:S(2)}) collective-permute-start(bf16[78592]{0:T(1024)(128)(2,1)S(1)} %pad_maximum_fusion.3), channel_id=1, source_target_pairs={{0,16},{1,17},{2,18},{3,19},{4,20},{5,21},{6,22},{7,23},{8,24},{9,... | collective-permute-start | bytes 471560 | tf_op jit(solution)/shard_map/ppermute | solution.py:160
  381.1 8.3 %collective-permute-start.7 = (bf16[45824]{0:T(1024)(128)(2,1)S(1)}, bf16[45824]{0:T(1024)(128)(2,1)S(1)}, u32[]{:S(2)}, u32[]{:S(2)}) collective-permute-start(bf16[45824]{0:T(1024)(128)(2,1)S(1)} %pad_maximum_fusion.4), channel_id=1, source_target_pairs={{0,4},{1,5},{2,6},{3,7},{4,0},{5,1},{6,2},{7,3},{8,12},{9,13},{10,... | collective-permute-start | bytes 274952 | tf_op jit(solution)/shard_map/ppermute | solution.py:160
  389.8 7.6 %collective-permute-start.8 = (bf16[29440]{0:T(1024)(128)(2,1)S(1)}, bf16[29440]{0:T(1024)(128)(2,1)S(1)}, u32[]{:S(2)}, u32[]{:S(2)}) collective-permute-start(bf16[29440]{0:T(1024)(128)(2,1)S(1)} %pad_maximum_fusion.5), channel_id=1, source_target_pairs={{0,32},{1,33},{2,34},{3,35},{4,36},{5,37},{6,38},{7,39},{8,40},{9,... | collective-permute-start | bytes 176648 | tf_op jit(solution)/shard_map/ppermute | solution.py:160
  397.7 9.8 %collective-permute-start.9 = (bf16[21248]{0:T(1024)(128)(2,1)S(1)}, bf16[21248]{0:T(1024)(128)(2,1)S(1)}, u32[]{:S(2)}, u32[]{:S(2)}) collective-permute-start(bf16[21248]{0:T(1024)(128)(2,1)S(1)} %pad_maximum_fusion.6), channel_id=1, source_target_pairs={{0,8},{1,9},{2,10},{3,11},{4,12},{5,13},{6,14},{7,15},{8,0},{9,1},... | collective-permute-start | bytes 127496 | tf_op jit(solution)/shard_map/ppermute | solution.py:160
  (107 other events, 244.1 us)

commit v3 on v2

--- a/solution.py
+++ b/solution.py
@@ -57,6 +57,9 @@
         normalized_input.reshape(-1, channels), proj_in, preferred_element_type=jnp.float32
     )
     hidden_expanded = jax.nn.gelu(channel_mixed, approximate=False).astype(jnp.bfloat16)
+    slope = 0.5 * (1.0 + lax.erf(channel_mixed * (1.0 / math.sqrt(2.0)))) + channel_mixed * jnp.exp(
+        -0.5 * channel_mixed * channel_mixed
+    ) * (1.0 / math.sqrt(2.0 * math.pi))
     residual_return = jnp.dot(
         hidden_expanded, proj_out, preferred_element_type=jnp.float32
     ).reshape(lead + (channels,))
@@ -67,7 +70,7 @@
             standardized_input,
             inverse_deviation,
             normalized_input,
-            channel_mixed,
+            slope,
             hidden_expanded,
             residual_return,
         ),
@@ -80,7 +83,7 @@
         standardized_input,
         inverse_deviation,
         normalized_input,
-        channel_mixed,
+        slope,
         hidden_expanded,
         residual_return,
     ) = saved_residuals
@@ -97,9 +100,6 @@
         .astype(jnp.bfloat16)
         .astype(jnp.float32)
     )
-    slope = 0.5 * (1.0 + lax.erf(channel_mixed * (1.0 / math.sqrt(2.0)))) + channel_mixed * jnp.exp(
-        -0.5 * channel_mixed * channel_mixed
-    ) * (1.0 / math.sqrt(2.0 * math.pi))
     ct_mixed = (ct_hidden * slope).astype(jnp.bfloat16)
     g_in = jnp.dot(
         ct_mixed.T, normalized_input.reshape(-1, channels), preferred_element_type=jnp.float32
@@ -183,9 +183,11 @@
     holder = view_slot // slot_dev
     local_row = view_slot % slot_dev
     side = holder - holder_id + 1
-    extended = padded_2(scene_grad, (("dp", 0),), slot_dev)
-    rows = side * slot_dev + local_row
-    targets = jnp.take(extended, rows, axis=0)
+    from_left = from_behind(scene_grad[2 * views : 3 * views], "dp", 1)
+    from_right = from_behind(scene_grad[0:views], "dp", -1)
+    candidates = jnp.concatenate([from_left, scene_grad[views : 2 * views], from_right])
+    rows = side * views + local_row - (2 - side) * views
+    targets = jnp.take(candidates, rows, axis=0)
     ticks = views + sections - 1
     empty_map = jnp.zeros(images.shape[1:], jnp.bfloat16)
 

time: 414 us -> 551 us (1.33); the launches traced: 411 us -> 541 us
  local copies, waits for them, and re-layouts: 68.5 us -> 143 us
  other arithmetic: 135 us -> 205 us
  waiting for transfers between devices: 59.6 us -> 36.4 us
  matrix products: 67.8 us -> 75.9 us
    slice x27, local copies, waits for them, and re-layouts: 0.4 us -> 37.6 us  [depthwise(): kernel[row_tap * ksize + col_tap]]
    slice x27, local copies, waits for them, and re-layouts: 17.1 us -> 44.1 us  [block_backward(): kernel[row_tap * ksize + col_tap]]
    dynamic_update_slice x36 -> x45, other arithmetic: 28.2 us -> 54 us  [forward_tick(): lax.dynamic_update_index_in_dim(buf, val, index, 0)]
    ppermute x18 -> x20, waiting for transfers between devices: 37.7 us -> 15.2 us  [from_behind(): return lax.ppermute(block, axis, route)]
    dot_general x9, matrix products: 2.89 us -> 12.3 us  [block_backward(): jnp.dot(ct_mixed, proj_in.T, preferred_element_type=jnp.float32)]
    reduce_sum x9, other arithmetic: 5.31 us -> 14.4 us  [block_backward(): jnp.sum(normalized_cotangent * standardized_input, axis=(0, 1, 2))]
    dynamic_update_slice x9 -> x0, local copies, waits for them, and re-layouts: 7.96 us -> none  [forward_tick(): lax.dynamic_update_index_in_dim(buf, val, index, 0)]
    reduce_sum x9, other arithmetic: 11.9 us -> 18.9 us  [block_forward(): centered_input = jnp.mean(depthwise_output, axis=-1, keepdims=True)]
where the time goes in v3:
time: 551 us; the launch traced here: 541 us
  other arithmetic  205 us (37%)
  local copies, waits for them, and re-layouts  143 us (26%)
  matrix products  75.9 us (14%)
  starting transfers between devices  75.2 us (14%)
  waiting for transfers between devices  36.4 us (7%)
    dynamic_update_slice x45, other arithmetic, forward_tick(): lax.dynamic_update_index_in_dim(buf, val, index, 0)  54 us
    ppermute x20, starting transfers between devices, from_behind(): return lax.ppermute(block, axis, route)  46.5 us
    slice x27, local copies, waits for them, and re-layouts, block_backward(): kernel[row_tap * ksize + col_tap]  44.1 us
    slice x27, local copies, waits for them, and re-layouts, depthwise(): kernel[row_tap * ksize + col_tap]  37.6 us
    dot_general x9, matrix products, block_forward(): jnp.dot(normalized_input.reshape(-1, channels), proj_in, preferred_elemen...  29.4 us
    ppermute x6, starting transfers between devices, dp_reduce(): got = lax.ppermute(packet, axis, pairs).astype(jnp.float32)  28.7 us
    reduce_sum x27, other arithmetic, block_backward(): kernel_rows.append(jnp.sum(depthwise_cotangent * window, axis=(0, 1, 2)))  25 us
    ppermute x6, waiting for transfers between devices, dp_reduce(): got = lax.ppermute(packet, axis, pairs).astype(jnp.float32)  21.2 us
  transfers between devices with their start and end apart: 26, of which 15 were waited for; matrix products, arithmetic and copies ran while one was open for 16% of the time, Pallas kernels for 0%

profile of v3, /device:TPU:448, one launch (start us, length us, event | category | flops | bytes accessed | tf_op | source)
XLA Modules:
  0.0 541.0 jit_solution(11728621015417348351)
XLA Ops:
  18.2 186.1 %while.55 = (s32[]{:T(128)}, bf16[12,12,256]{2,1,0:T(8,128)(2,1)}, bf16[3,12,12,256]{3,2,1,0:T(8,128)(2,1)S(1)}, f32[3,1,12,12,256]{4,3,2,1,0:T(8,128)}, f32[3,1...) while((s32[]{:T(128)}, bf16[12,12,256]{2,1,0:T(8,128)(2,1)}, ...), condition=%wide.region_3.4_spmd, body=%wide.region_0.3_spmd.sunk | while | flops 165962176 | bytes 7540882 | solution.py:222
  23.4 2.1 fusion.402
  26.6 3.3 bitcast_dynamic-update-slice_fusion.12
  33.0 2.1 fusion.405
  46.8 3.3 bitcast_dynamic-update-slice_fusion.12
  53.2 2.1 fusion.405
  67.2 3.3 bitcast_dynamic-update-slice_fusion.12
  73.5 2.1 fusion.405
  88.2 3.3 bitcast_dynamic-update-slice_fusion.12
  94.6 2.1 fusion.405
  108.6 3.3 bitcast_dynamic-update-slice_fusion.12
  115.0 2.1 fusion.405
  128.9 3.3 bitcast_dynamic-update-slice_fusion.12
  135.2 2.1 fusion.405
  149.1 3.3 bitcast_dynamic-update-slice_fusion.12
  155.5 2.1 fusion.405
  169.8 3.3 bitcast_dynamic-update-slice_fusion.12
  180.4 2.5 collective-permute-done
  191.2 3.3 bitcast_dynamic-update-slice_fusion.12
  201.8 2.5 collective-permute-done
  205.0 265.8 %while.56 = (s32[]{:T(128)}, bf16[12,12,256]{2,1,0:T(8,128)(2,1)}, f32[49,256]{1,0:T(8,128)}, f32[256]{0:T(256)}, f32[1024,256]{1,0:T(8,128)S(1)}, /*index=5*/f3...) while((s32[]{:T(128)}, bf16[12,12,256]{2,1,0:T(8,128)(2,1)}, ...), condition=%wide.region_58.59_spmd.clone, body=%wide.region_4.58_spmd.clone.sunk | while | flops 312325632 | bytes 14996536 | solution.py:251
  222.6 2.2 fusion.423
  224.8 5.8 %collective-permute-start.1 = (bf16[12,12,256]{2,1,0:T(8,128)(2,1)S(1)}, bf16[12,12,256]{2,1,0:T(8,128)(2,1)}, u32[]{:S(2)}, u32[]{:S(2)}) collective-permute-start(bf16[12,12,256]{2,1,0:T(8,128)(2,1)S(1)} %fusion.423), channel_id=1, source_target_pairs={{64,0},{128,64},{192,128},{256,192},{320,256},{384,320},{448,384},... | collective-permute-start | bytes 221192 | tf_op jit(solution)/shard_map/while/body/eval_jaxpr/ppermute | solution.py:27
  254.5 2.2 fusion.423
  256.7 5.2 collective-permute-start.1
  285.8 2.2 fusion.423
  288.1 5.2 collective-permute-start.1
  317.1 2.2 fusion.423
  319.4 3.4 collective-permute-start.1
  346.7 2.2 fusion.423
  348.9 2.2 collective-permute-start.1
  375.0 2.2 fusion.423
  377.2 2.2 collective-permute-start.1
  403.3 2.2 fusion.423
  405.5 2.8 collective-permute-start.1
  432.2 2.2 fusion.423
  460.3 2.2 fusion.423
  472.5 3.1 copy_dynamic-update-slice_fusion.1
  488.3 4.8 collective-permute-start.5
  493.7 6.6 %collective-permute-done.5 = bf16[144128]{0:T(1024)(128)(2,1)S(1)} collective-permute-done((bf16[144128]{0:T(1024)(128)(2,1)S(1)}, bf16[144128]{0:T(1024)(128)(2,1)S(1)}, u32[]{:S(2)}, u32[]{:S(2)}) %collective-permute-start.5) | collective-permute-done | bytes 288288 | tf_op jit(solution)/shard_map/ppermute | solution.py:160
  501.4 5.6 %collective-permute-start.6 = (bf16[78592]{0:T(1024)(128)(2,1)S(1)}, bf16[78592]{0:T(1024)(128)(2,1)S(1)}, u32[]{:S(2)}, u32[]{:S(2)}) collective-permute-start(bf16[78592]{0:T(1024)(128)(2,1)S(1)} %pad_maximum_fusion.3), channel_id=1, source_target_pairs={{0,16},{1,17},{2,18},{3,19},{4,20},{5,21},{6,22},{7,23},{8,24},{9,... | collective-permute-start | bytes 471560 | tf_op jit(solution)/shard_map/ppermute | solution.py:160
  507.0 3.5 collective-permute-done.6
  511.4 4.1 collective-permute-start.7
  515.6 4.1 collective-permute-done.7
  520.0 5.2 collective-permute-start.8
  525.2 2.4 collective-permute-done.8
  527.9 7.1 %collective-permute-start.9 = (bf16[21248]{0:T(1024)(128)(2,1)S(1)}, bf16[21248]{0:T(1024)(128)(2,1)S(1)}, u32[]{:S(2)}, u32[]{:S(2)}) collective-permute-start(bf16[21248]{0:T(1024)(128)(2,1)S(1)} %pad_maximum_fusion.6), channel_id=1, source_target_pairs={{0,8},{1,9},{2,10},{3,11},{4,12},{5,13},{6,14},{7,15},{8,0},{9,1},... | collective-permute-start | bytes 127496 | tf_op jit(solution)/shard_map/ppermute | solution.py:160
  535.1 2.7 collective-permute-done.9
  (888 shorter events, 388.5 us)
Async XLA Ops:
  1.8 8.7 %collective-permute-start.2 = (bf16[2,12,12,256]{3,2,1,0:T(8,128)(2,1)S(1)}, bf16[2,12,12,256]{3,2,1,0:T(8,128)(2,1)S(1)}, u32[]{:S(2)}, u32[]{:S(2)}) collective-permute-start(bf16[2,12,12,256]{3,2,1,0:T(8,128)(2,1)S(1)} %get-tuple-element.1267), channel_id=1, source_target_pairs={{0,1},{1,2},{2,3},{3,4},{4,5},{5,6},{6,7},{7,8},{8,9},{9,10},{10,1... | collective-permute-start | bytes 442376 | tf_op jit(solution)/shard_map/ppermute | solution.py:27
  3.6 7.0 %collective-permute-start.3 = (bf16[2,12,12,256]{3,2,1,0:T(8,128)(2,1)S(1)}, bf16[2,12,12,256]{3,2,1,0:T(8,128)(2,1)S(1)}, u32[]{:S(2)}, u32[]{:S(2)}) collective-permute-start(bf16[2,12,12,256]{3,2,1,0:T(8,128)(2,1)S(1)} %get-tuple-element.1268), channel_id=1, source_target_pairs={{1,0},{2,1},{3,2},{4,3},{5,4},{6,5},{7,6},{8,7},{9,8},{10,9},{11,1... | collective-permute-start | bytes 442376 | tf_op jit(solution)/shard_map/ppermute | solution.py:27
  18.2 11.6 %copy-start.12 = (f32[256]{0:T(256)}, f32[256]{0:T(256)S(1)}, u32[]{:S(2)}) copy-start(f32[256]{0:T(256)S(1)} %get-tuple-element.1897) | copy-start | bytes 3076 | tf_op jit(solution)/shard_map/while
  31.5 6.9 %collective-permute-start = (bf16[12,12,256]{2,1,0:T(8,128)(2,1)}, bf16[12,12,256]{2,1,0:T(8,128)(2,1)}, u32[]{:S(2)}, u32[]{:S(2)}) collective-permute-start(bf16[12,12,256]{2,1,0:T(8,128)(2,1)} %fusion.404), channel_id=1, source_target_pairs={{0,64},{64,128},{128,192},{192,256},{256,320},{320,384},{384,448},... | collective-permute-start | bytes 221192 | tf_op jit(solution)/shard_map/while/body/eval_jaxpr/ppermute | solution.py:27
  38.4 11.6 %copy-start.12 = (f32[256]{0:T(256)}, f32[256]{0:T(256)S(1)}, u32[]{:S(2)}) copy-start(f32[256]{0:T(256)S(1)} %get-tuple-element.1897) | copy-start | bytes 3076 | tf_op jit(solution)/shard_map/while
  51.7 7.1 %collective-permute-start = (bf16[12,12,256]{2,1,0:T(8,128)(2,1)}, bf16[12,12,256]{2,1,0:T(8,128)(2,1)}, u32[]{:S(2)}, u32[]{:S(2)}) collective-permute-start(bf16[12,12,256]{2,1,0:T(8,128)(2,1)} %fusion.404), channel_id=1, source_target_pairs={{0,64},{64,128},{128,192},{192,256},{256,320},{320,384},{384,448},... | collective-permute-start | bytes 221192 | tf_op jit(solution)/shard_map/while/body/eval_jaxpr/ppermute | solution.py:27
  58.8 11.6 %copy-start.12 = (f32[256]{0:T(256)}, f32[256]{0:T(256)S(1)}, u32[]{:S(2)}) copy-start(f32[256]{0:T(256)S(1)} %get-tuple-element.1897) | copy-start | bytes 3076 | tf_op jit(solution)/shard_map/while
  72.1 7.8 %collective-permute-start = (bf16[12,12,256]{2,1,0:T(8,128)(2,1)}, bf16[12,12,256]{2,1,0:T(8,128)(2,1)}, u32[]{:S(2)}, u32[]{:S(2)}) collective-permute-start(bf16[12,12,256]{2,1,0:T(8,128)(2,1)} %fusion.404), channel_id=1, source_target_pairs={{0,64},{64,128},{128,192},{192,256},{256,320},{320,384},{384,448},... | collective-permute-start | bytes 221192 | tf_op jit(solution)/shard_map/while/body/eval_jaxpr/ppermute | solution.py:27
  79.9 11.6 %copy-start.12 = (f32[256]{0:T(256)}, f32[256]{0:T(256)S(1)}, u32[]{:S(2)}) copy-start(f32[256]{0:T(256)S(1)} %get-tuple-element.1897) | copy-start | bytes 3076 | tf_op jit(solution)/shard_map/while
  93.1 7.2 %collective-permute-start = (bf16[12,12,256]{2,1,0:T(8,128)(2,1)}, bf16[12,12,256]{2,1,0:T(8,128)(2,1)}, u32[]{:S(2)}, u32[]{:S(2)}) collective-permute-start(bf16[12,12,256]{2,1,0:T(8,128)(2,1)} %fusion.404), channel_id=1, source_target_pairs={{0,64},{64,128},{128,192},{192,256},{256,320},{320,384},{384,448},... | collective-permute-start | bytes 221192 | tf_op jit(solution)/shard_map/while/body/eval_jaxpr/ppermute | solution.py:27
  100.3 11.6 %copy-start.12 = (f32[256]{0:T(256)}, f32[256]{0:T(256)S(1)}, u32[]{:S(2)}) copy-start(f32[256]{0:T(256)S(1)} %get-tuple-element.1897) | copy-start | bytes 3076 | tf_op jit(solution)/shard_map/while
  113.6 6.9 %collective-permute-start = (bf16[12,12,256]{2,1,0:T(8,128)(2,1)}, bf16[12,12,256]{2,1,0:T(8,128)(2,1)}, u32[]{:S(2)}, u32[]{:S(2)}) collective-permute-start(bf16[12,12,256]{2,1,0:T(8,128)(2,1)} %fusion.404), channel_id=1, source_target_pairs={{0,64},{64,128},{128,192},{192,256},{256,320},{320,384},{384,448},... | collective-permute-start | bytes 221192 | tf_op jit(solution)/shard_map/while/body/eval_jaxpr/ppermute | solution.py:27
  120.5 11.6 %copy-start.12 = (f32[256]{0:T(256)}, f32[256]{0:T(256)S(1)}, u32[]{:S(2)}) copy-start(f32[256]{0:T(256)S(1)} %get-tuple-element.1897) | copy-start | bytes 3076 | tf_op jit(solution)/shard_map/while
  133.8 6.9 %collective-permute-start = (bf16[12,12,256]{2,1,0:T(8,128)(2,1)}, bf16[12,12,256]{2,1,0:T(8,128)(2,1)}, u32[]{:S(2)}, u32[]{:S(2)}) collective-permute-start(bf16[12,12,256]{2,1,0:T(8,128)(2,1)} %fusion.404), channel_id=1, source_target_pairs={{0,64},{64,128},{128,192},{192,256},{256,320},{320,384},{384,448},... | collective-permute-start | bytes 221192 | tf_op jit(solution)/shard_map/while/body/eval_jaxpr/ppermute | solution.py:27
  140.7 11.6 %copy-start.12 = (f32[256]{0:T(256)}, f32[256]{0:T(256)S(1)}, u32[]{:S(2)}) copy-start(f32[256]{0:T(256)S(1)} %get-tuple-element.1897) | copy-start | bytes 3076 | tf_op jit(solution)/shard_map/while
  154.0 7.5 %collective-permute-start = (bf16[12,12,256]{2,1,0:T(8,128)(2,1)}, bf16[12,12,256]{2,1,0:T(8,128)(2,1)}, u32[]{:S(2)}, u32[]{:S(2)}) collective-permute-start(bf16[12,12,256]{2,1,0:T(8,128)(2,1)} %fusion.404), channel_id=1, source_target_pairs={{0,64},{64,128},{128,192},{192,256},{256,320},{320,384},{384,448},... | collective-permute-start | bytes 221192 | tf_op jit(solution)/shard_map/while/body/eval_jaxpr/ppermute | solution.py:27
  161.5 11.6 %copy-start.12 = (f32[256]{0:T(256)}, f32[256]{0:T(256)S(1)}, u32[]{:S(2)}) copy-start(f32[256]{0:T(256)S(1)} %get-tuple-element.1897) | copy-start | bytes 3076 | tf_op jit(solution)/shard_map/while
  174.7 8.1 %collective-permute-start = (bf16[12,12,256]{2,1,0:T(8,128)(2,1)}, bf16[12,12,256]{2,1,0:T(8,128)(2,1)}, u32[]{:S(2)}, u32[]{:S(2)}) collective-permute-start(bf16[12,12,256]{2,1,0:T(8,128)(2,1)} %fusion.404), channel_id=1, source_target_pairs={{0,64},{64,128},{128,192},{192,256},{256,320},{320,384},{384,448},... | collective-permute-start | bytes 221192 | tf_op jit(solution)/shard_map/while/body/eval_jaxpr/ppermute | solution.py:27
  182.9 11.6 %copy-start.12 = (f32[256]{0:T(256)}, f32[256]{0:T(256)S(1)}, u32[]{:S(2)}) copy-start(f32[256]{0:T(256)S(1)} %get-tuple-element.1897) | copy-start | bytes 3076 | tf_op jit(solution)/shard_map/while
  196.1 8.2 %collective-permute-start = (bf16[12,12,256]{2,1,0:T(8,128)(2,1)}, bf16[12,12,256]{2,1,0:T(8,128)(2,1)}, u32[]{:S(2)}, u32[]{:S(2)}) collective-permute-start(bf16[12,12,256]{2,1,0:T(8,128)(2,1)} %fusion.404), channel_id=1, source_target_pairs={{0,64},{64,128},{128,192},{192,256},{256,320},{320,384},{384,448},... | collective-permute-start | bytes 221192 | tf_op jit(solution)/shard_map/while/body/eval_jaxpr/ppermute | solution.py:27
  219.0 14.4 %copy-start.6 = (f32[49,256]{1,0:T(8,128)S(1)}, f32[49,256]{1,0:T(8,128)}, u32[]{:S(2)}) copy-start(f32[49,256]{1,0:T(8,128)} %get-tuple-element.1932) | copy-start | bytes 150532 | tf_op jit(solution)/shard_map/while
  224.8 11.5 %collective-permute-start.1 = (bf16[12,12,256]{2,1,0:T(8,128)(2,1)S(1)}, bf16[12,12,256]{2,1,0:T(8,128)(2,1)}, u32[]{:S(2)}, u32[]{:S(2)}) collective-permute-start(bf16[12,12,256]{2,1,0:T(8,128)(2,1)S(1)} %fusion.423), channel_id=1, source_target_pairs={{64,0},{128,64},{192,128},{256,192},{320,256},{384,320},{448,384},... | collective-permute-start | bytes 221192 | tf_op jit(solution)/shard_map/while/body/eval_jaxpr/ppermute | solution.py:27
  236.9 8.7 %copy-start.14 = (f32[256]{0:T(256)}, f32[256]{0:T(256)S(1)}, u32[]{:S(2)}) copy-start(f32[256]{0:T(256)S(1)} %get-tuple-element.1970) | copy-start | bytes 3076 | tf_op jit(solution)/shard_map/while
  250.9 13.8 %copy-start.6 = (f32[49,256]{1,0:T(8,128)S(1)}, f32[49,256]{1,0:T(8,128)}, u32[]{:S(2)}) copy-start(f32[49,256]{1,0:T(8,128)} %get-tuple-element.1932) | copy-start | bytes 150532 | tf_op jit(solution)/shard_map/while
  256.7 10.9 %collective-permute-start.1 = (bf16[12,12,256]{2,1,0:T(8,128)(2,1)S(1)}, bf16[12,12,256]{2,1,0:T(8,128)(2,1)}, u32[]{:S(2)}, u32[]{:S(2)}) collective-permute-start(bf16[12,12,256]{2,1,0:T(8,128)(2,1)S(1)} %fusion.423), channel_id=1, source_target_pairs={{64,0},{128,64},{192,128},{256,192},{320,256},{384,320},{448,384},... | collective-permute-start | bytes 221192 | tf_op jit(solution)/shard_map/while/body/eval_jaxpr/ppermute | solution.py:27
  268.2 8.7 %copy-start.14 = (f32[256]{0:T(256)}, f32[256]{0:T(256)S(1)}, u32[]{:S(2)}) copy-start(f32[256]{0:T(256)S(1)} %get-tuple-element.1970) | copy-start | bytes 3076 | tf_op jit(solution)/shard_map/while
  282.2 13.8 %copy-start.6 = (f32[49,256]{1,0:T(8,128)S(1)}, f32[49,256]{1,0:T(8,128)}, u32[]{:S(2)}) copy-start(f32[49,256]{1,0:T(8,128)} %get-tuple-element.1932) | copy-start | bytes 150532 | tf_op jit(solution)/shard_map/while
  288.1 10.9 %collective-permute-start.1 = (bf16[12,12,256]{2,1,0:T(8,128)(2,1)S(1)}, bf16[12,12,256]{2,1,0:T(8,128)(2,1)}, u32[]{:S(2)}, u32[]{:S(2)}) collective-permute-start(bf16[12,12,256]{2,1,0:T(8,128)(2,1)S(1)} %fusion.423), channel_id=1, source_target_pairs={{64,0},{128,64},{192,128},{256,192},{320,256},{384,320},{448,384},... | collective-permute-start | bytes 221192 | tf_op jit(solution)/shard_map/while/body/eval_jaxpr/ppermute | solution.py:27
  299.5 8.7 %copy-start.14 = (f32[256]{0:T(256)}, f32[256]{0:T(256)S(1)}, u32[]{:S(2)}) copy-start(f32[256]{0:T(256)S(1)} %get-tuple-element.1970) | copy-start | bytes 3076 | tf_op jit(solution)/shard_map/while
  313.5 12.0 %copy-start.6 = (f32[49,256]{1,0:T(8,128)S(1)}, f32[49,256]{1,0:T(8,128)}, u32[]{:S(2)}) copy-start(f32[49,256]{1,0:T(8,128)} %get-tuple-element.1932) | copy-start | bytes 150532 | tf_op jit(solution)/shard_map/while
  319.4 9.1 %collective-permute-start.1 = (bf16[12,12,256]{2,1,0:T(8,128)(2,1)S(1)}, bf16[12,12,256]{2,1,0:T(8,128)(2,1)}, u32[]{:S(2)}, u32[]{:S(2)}) collective-permute-start(bf16[12,12,256]{2,1,0:T(8,128)(2,1)S(1)} %fusion.423), channel_id=1, source_target_pairs={{64,0},{128,64},{192,128},{256,192},{320,256},{384,320},{448,384},... | collective-permute-start | bytes 221192 | tf_op jit(solution)/shard_map/while/body/eval_jaxpr/ppermute | solution.py:27
  343.1 10.8 %copy-start.6 = (f32[49,256]{1,0:T(8,128)S(1)}, f32[49,256]{1,0:T(8,128)}, u32[]{:S(2)}) copy-start(f32[49,256]{1,0:T(8,128)} %get-tuple-element.1932) | copy-start | bytes 150532 | tf_op jit(solution)/shard_map/while
  348.9 7.9 %collective-permute-start.1 = (bf16[12,12,256]{2,1,0:T(8,128)(2,1)S(1)}, bf16[12,12,256]{2,1,0:T(8,128)(2,1)}, u32[]{:S(2)}, u32[]{:S(2)}) collective-permute-start(bf16[12,12,256]{2,1,0:T(8,128)(2,1)S(1)} %fusion.423), channel_id=1, source_target_pairs={{64,0},{128,64},{192,128},{256,192},{320,256},{384,320},{448,384},... | collective-permute-start | bytes 221192 | tf_op jit(solution)/shard_map/while/body/eval_jaxpr/ppermute | solution.py:27
  357.3 8.7 %copy-start.14 = (f32[256]{0:T(256)}, f32[256]{0:T(256)S(1)}, u32[]{:S(2)}) copy-start(f32[256]{0:T(256)S(1)} %get-tuple-element.1970) | copy-start | bytes 3076 | tf_op jit(solution)/shard_map/while
  371.4 10.8 %copy-start.6 = (f32[49,256]{1,0:T(8,128)S(1)}, f32[49,256]{1,0:T(8,128)}, u32[]{:S(2)}) copy-start(f32[49,256]{1,0:T(8,128)} %get-tuple-element.1932) | copy-start | bytes 150532 | tf_op jit(solution)/shard_map/while
  377.2 7.9 %collective-permute-start.1 = (bf16[12,12,256]{2,1,0:T(8,128)(2,1)S(1)}, bf16[12,12,256]{2,1,0:T(8,128)(2,1)}, u32[]{:S(2)}, u32[]{:S(2)}) collective-permute-start(bf16[12,12,256]{2,1,0:T(8,128)(2,1)S(1)} %fusion.423), channel_id=1, source_target_pairs={{64,0},{128,64},{192,128},{256,192},{320,256},{384,320},{448,384},... | collective-permute-start | bytes 221192 | tf_op jit(solution)/shard_map/while/body/eval_jaxpr/ppermute | solution.py:27
  399.7 11.4 %copy-start.6 = (f32[49,256]{1,0:T(8,128)S(1)}, f32[49,256]{1,0:T(8,128)}, u32[]{:S(2)}) copy-start(f32[49,256]{1,0:T(8,128)} %get-tuple-element.1932) | copy-start | bytes 150532 | tf_op jit(solution)/shard_map/while
  405.5 8.5 %collective-permute-start.1 = (bf16[12,12,256]{2,1,0:T(8,128)(2,1)S(1)}, bf16[12,12,256]{2,1,0:T(8,128)(2,1)}, u32[]{:S(2)}, u32[]{:S(2)}) collective-permute-start(bf16[12,12,256]{2,1,0:T(8,128)(2,1)S(1)} %fusion.423), channel_id=1, source_target_pairs={{64,0},{128,64},{192,128},{256,192},{320,256},{384,320},{448,384},... | collective-permute-start | bytes 221192 | tf_op jit(solution)/shard_map/while/body/eval_jaxpr/ppermute | solution.py:27
  428.6 10.6 %copy-start.6 = (f32[49,256]{1,0:T(8,128)S(1)}, f32[49,256]{1,0:T(8,128)}, u32[]{:S(2)}) copy-start(f32[49,256]{1,0:T(8,128)} %get-tuple-element.1932) | copy-start | bytes 150532 | tf_op jit(solution)/shard_map/while
  434.4 7.7 %collective-permute-start.1 = (bf16[12,12,256]{2,1,0:T(8,128)(2,1)S(1)}, bf16[12,12,256]{2,1,0:T(8,128)(2,1)}, u32[]{:S(2)}, u32[]{:S(2)}) collective-permute-start(bf16[12,12,256]{2,1,0:T(8,128)(2,1)S(1)} %fusion.423), channel_id=1, source_target_pairs={{64,0},{128,64},{192,128},{256,192},{320,256},{384,320},{448,384},... | collective-permute-start | bytes 221192 | tf_op jit(solution)/shard_map/while/body/eval_jaxpr/ppermute | solution.py:27
  456.7 10.6 %copy-start.6 = (f32[49,256]{1,0:T(8,128)S(1)}, f32[49,256]{1,0:T(8,128)}, u32[]{:S(2)}) copy-start(f32[49,256]{1,0:T(8,128)} %get-tuple-element.1932) | copy-start | bytes 150532 | tf_op jit(solution)/shard_map/while
  462.5 7.7 %collective-permute-start.1 = (bf16[12,12,256]{2,1,0:T(8,128)(2,1)S(1)}, bf16[12,12,256]{2,1,0:T(8,128)(2,1)}, u32[]{:S(2)}, u32[]{:S(2)}) collective-permute-start(bf16[12,12,256]{2,1,0:T(8,128)(2,1)S(1)} %fusion.423), channel_id=1, source_target_pairs={{64,0},{128,64},{192,128},{256,192},{320,256},{384,320},{448,384},... | collective-permute-start | bytes 221192 | tf_op jit(solution)/shard_map/while/body/eval_jaxpr/ppermute | solution.py:27
  480.1 3.8 collective-permute-start.4
  488.3 11.9 %collective-permute-start.5 = (bf16[144128]{0:T(1024)(128)(2,1)S(1)}, bf16[144128]{0:T(1024)(128)(2,1)S(1)}, u32[]{:S(2)}, u32[]{:S(2)}) collective-permute-start(bf16[144128]{0:T(1024)(128)(2,1)S(1)} %pad_maximum_fusion.2), channel_id=1, source_target_pairs={{0,2},{1,3},{2,0},{3,1},{4,6},{5,7},{6,4},{7,5},{8,10},{9,11},{10,... | collective-permute-start | bytes 864776 | tf_op jit(solution)/shard_map/ppermute | solution.py:160
  501.4 9.1 %collective-permute-start.6 = (bf16[78592]{0:T(1024)(128)(2,1)S(1)}, bf16[78592]{0:T(1024)(128)(2,1)S(1)}, u32[]{:S(2)}, u32[]{:S(2)}) collective-permute-start(bf16[78592]{0:T(1024)(128)(2,1)S(1)} %pad_maximum_fusion.3), channel_id=1, source_target_pairs={{0,16},{1,17},{2,18},{3,19},{4,20},{5,21},{6,22},{7,23},{8,24},{9,... | collective-permute-start | bytes 471560 | tf_op jit(solution)/shard_map/ppermute | solution.py:160
  511.4 8.3 %collective-permute-start.7 = (bf16[45824]{0:T(1024)(128)(2,1)S(1)}, bf16[45824]{0:T(1024)(128)(2,1)S(1)}, u32[]{:S(2)}, u32[]{:S(2)}) collective-permute-start(bf16[45824]{0:T(1024)(128)(2,1)S(1)} %pad_maximum_fusion.4), channel_id=1, source_target_pairs={{0,4},{1,5},{2,6},{3,7},{4,0},{5,1},{6,2},{7,3},{8,12},{9,13},{10,... | collective-permute-start | bytes 274952 | tf_op jit(solution)/shard_map/ppermute | solution.py:160
  520.0 7.6 %collective-permute-start.8 = (bf16[29440]{0:T(1024)(128)(2,1)S(1)}, bf16[29440]{0:T(1024)(128)(2,1)S(1)}, u32[]{:S(2)}, u32[]{:S(2)}) collective-permute-start(bf16[29440]{0:T(1024)(128)(2,1)S(1)} %pad_maximum_fusion.5), channel_id=1, source_target_pairs={{0,32},{1,33},{2,34},{3,35},{4,36},{5,37},{6,38},{7,39},{8,40},{9,... | collective-permute-start | bytes 176648 | tf_op jit(solution)/shard_map/ppermute | solution.py:160
  527.9 9.8 %collective-permute-start.9 = (bf16[21248]{0:T(1024)(128)(2,1)S(1)}, bf16[21248]{0:T(1024)(128)(2,1)S(1)}, u32[]{:S(2)}, u32[]{:S(2)}) collective-permute-start(bf16[21248]{0:T(1024)(128)(2,1)S(1)} %pad_maximum_fusion.6), channel_id=1, source_target_pairs={{0,8},{1,9},{2,10},{3,11},{4,12},{5,13},{6,14},{7,15},{8,0},{9,1},... | collective-permute-start | bytes 127496 | tf_op jit(solution)/shard_map/ppermute | solution.py:160
  (162 other events, 471.0 us)

commit v4 on v2

--- a/solution.py
+++ b/solution.py
@@ -149,18 +149,41 @@
     big = jnp.stack([g_in_t, g_out]).reshape((2,) + (2,) * bits + (share * channels,))
     remaining = list(range(bits - 1, -1, -1))
     order = [0] + [b for b in (1, 4, 2, 5, 3) if b < bits] + [b for b in range(6, bits)]
-    for bit in order:
-        position = remaining.index(bit) + 1
-        mine = (me >> bit) & 1
-        keep = lax.dynamic_index_in_dim(big, mine, position, keepdims=False)
-        send = lax.dynamic_index_in_dim(big, 1 - mine, position, keepdims=False)
+    groups = [order[i : i + 2] for i in range(0, len(order), 2)]
+    for group in groups:
+        positions = [remaining.index(b) + 1 for b in group]
+        mine = [(me >> b) & 1 for b in group]
+
+        def chunk(values, big=big, positions=positions):
+            part = big
+            for p, v in sorted(zip(positions, values), key=lambda t: -t[0]):
+                part = lax.dynamic_index_in_dim(part, v, p, keepdims=False)
+            return part
+
+        keep = chunk(mine)
         small = small.astype(jnp.bfloat16).astype(jnp.float32)
-        packet = jnp.concatenate([send.reshape(-1), small]).astype(jnp.bfloat16)
-        pairs = [(d, d ^ (1 << bit)) for d in range(holders)]
-        got = lax.ppermute(packet, axis, pairs).astype(jnp.float32)
-        big = keep + got[: keep.size].reshape(keep.shape)
-        small = small + got[keep.size :]
-        remaining.pop(position - 1)
+        received = [None]
+        for code in range(1, 1 << len(group)):
+            flips = [(code >> j) & 1 for j in range(len(group))]
+            send = chunk([m ^ f for m, f in zip(mine, flips)])
+            packet = jnp.concatenate([send.reshape(-1), small]).astype(jnp.bfloat16)
+            mask = sum(f << b for f, b in zip(flips, group))
+            pairs = [(d, d ^ mask) for d in range(holders)]
+            received.append(lax.ppermute(packet, axis, pairs).astype(jnp.float32))
+        big = keep
+        for got in received[1:]:
+            big = big + got[: keep.size].reshape(keep.shape)
+        stacked = jnp.stack([small] + [got[keep.size :] for got in received[1:]])
+        my_code = sum(m << j for j, m in enumerate(mine))
+        terms = [
+            lax.dynamic_index_in_dim(stacked, my_code ^ a, 0, keepdims=False)
+            for a in range(1 << len(group))
+        ]
+        while len(terms) > 1:
+            terms = [terms[i] + terms[i + 1] for i in range(0, len(terms), 2)]
+        small = terms[0]
+        for b in group:
+            remaining.remove(b)
     big = big.reshape(2, share, channels)
     return big[0].T, big[1], small
 

time: 414 us -> 461 us (1.11)
  other arithmetic: 135 us -> 162 us
  local copies, waits for them, and re-layouts: 68.5 us -> 78 us
  matrix products: 67.8 us -> 77 us
  waiting for transfers between devices: 59.6 us -> 52 us
  starting transfers between devices: 75.2 us -> 80.4 us
    dynamic_update_slice x36, other arithmetic: 28.2 us -> 45.7 us  [forward_tick(): lax.dynamic_update_index_in_dim(buf, val, index, 0)]
    ppermute x18, waiting for transfers between devices: 37.7 us -> 25.4 us  [from_behind(): return lax.ppermute(block, axis, route)]
    dot_general x9, matrix products: 2.89 us -> 12.3 us  [block_backward(): jnp.dot(ct_mixed, proj_in.T, preferred_element_type=jnp.float32)]
    mul x9, local copies, waits for them, and re-layouts: 0.09 us -> 6.34 us  [block_backward(): inverse_deviation * (standardized_cotangent - jnp.mean(standardized_cotan...]
    convert_element_type x9, other arithmetic: 0.18 us -> 6.27 us  [block_backward(): ct_back = (incoming * scale).astype(jnp.bfloat16).reshape(-1, channels)]
    reduce_sum x27, other arithmetic: 19.1 us -> 25 us  [block_backward(): kernel_rows.append(jnp.sum(depthwise_cotangent * window, axis=(0, 1, 2)))]
    while x252 -> x522, local copies, waits for them, and re-layouts: 5.45 us -> 11.2 us
    ppermute x6 -> x9, starting transfers between devices: 31.4 us -> 37.1 us  [dp_reduce(): received.append(lax.ppermute(packet, axis, pairs).astype(jnp.float32))]
  transfers between devices with their start and end apart: 26 -> 29, of which waited for: 15 -> 15; matrix products, arithmetic and copies ran while one was open for 16% -> 17% of each run, Pallas kernels for 0% -> 0%
where the time goes in v4:
time: 461 us; the launch traced here: 457 us
  other arithmetic  162 us (35%)
  starting transfers between devices  80.4 us (17%)
  local copies, waits for them, and re-layouts  78 us (17%)
  matrix products  77 us (17%)
  waiting for transfers between devices  52 us (11%)
  loops' own time  6.03 us (1%)
    dynamic_update_slice x36, other arithmetic, forward_tick(): lax.dynamic_update_index_in_dim(buf, val, index, 0)  45.7 us
    ppermute x18, starting transfers between devices, from_behind(): return lax.ppermute(block, axis, route)  40.2 us
    ppermute x9, starting transfers between devices, dp_reduce(): received.append(lax.ppermute(packet, axis, pairs).astype(jnp.float32))  37.1 us
    dot_general x9, matrix products, block_forward(): jnp.dot(normalized_input.reshape(-1, channels), proj_in, preferred_elemen...  29 us
    ppermute x9, waiting for transfers between devices, dp_reduce(): received.append(lax.ppermute(packet, axis, pairs).astype(jnp.float32))  26.5 us
    ppermute x18, waiting for transfers between devices, from_behind(): return lax.ppermute(block, axis, route)  25.4 us
    reduce_sum x27, other arithmetic, block_backward(): kernel_rows.append(jnp.sum(depthwise_cotangent * window, axis=(0, 1, 2)))  25 us
    squeeze x9, other arithmetic, backward_step(): return (back_x[0], back_p)  18.7 us
  transfers between devices with their start and end apart: 29, of which 15 were waited for; matrix products, arithmetic and copies ran while one was open for 17% of the time, Pallas kernels for 0%

profile of v4, /device:TPU:448, one launch (start us, length us, event | category | flops | bytes accessed | tf_op | source)
XLA Modules:
  0.0 456.5 jit_solution(922248857576493336)
XLA Ops:
  9.4 2.5 pad_maximum_fusion
  21.1 149.5 %while.55 = (s32[]{:T(128)}, bf16[12,12,256]{2,1,0:T(8,128)(2,1)S(1)}, bf16[3,12,12,256]{3,2,1,0:T(8,128)(2,1)}, f32[3,1,12,12,256]{4,3,2,1,0:T(8,128)}, f32[3,1...) while((s32[]{:T(128)}, ...), condition=%wide.region_3.4_spmd, body=%wide.region_0.3_spmd.sunk | while | flops 164782528 | bytes 9619837 | solution.py:243
  26.4 3.2 bitcast_dynamic-update-slice_fusion.14
  34.9 2.4 collective-permute-done
  42.6 3.2 bitcast_dynamic-update-slice_fusion.14
  51.1 2.4 collective-permute-done
  58.8 3.2 bitcast_dynamic-update-slice_fusion.14
  67.3 2.4 collective-permute-done
  74.9 3.2 bitcast_dynamic-update-slice_fusion.14
  83.4 2.4 collective-permute-done
  91.1 3.2 bitcast_dynamic-update-slice_fusion.14
  99.6 2.8 collective-permute-done
  107.7 3.2 bitcast_dynamic-update-slice_fusion.14
  116.2 2.9 collective-permute-done
  124.5 3.2 bitcast_dynamic-update-slice_fusion.14
  132.9 3.5 collective-permute-done
  141.7 3.2 bitcast_dynamic-update-slice_fusion.14
  150.1 3.6 collective-permute-done
  159.1 3.2 bitcast_dynamic-update-slice_fusion.14
  167.6 3.0 collective-permute-done
  170.6 204.7 %while.56 = (s32[]{:T(128)}, bf16[12,12,256]{2,1,0:T(8,128)(2,1)S(1)}, f32[49,256]{1,0:T(8,128)S(1)}, f32[256]{0:T(256)}, f32[1024,256]{1,0:T(8,128)S(1)}, /*ind...) while((s32[]{:T(128)}, ...), condition=%wide.region_58.59_spmd.clone, body=%wide.region_4.58_spmd.clone.sunk | while | flops 313505280 | bytes 12309896 | solution.py:272
  182.6 2.1 fusion.421
  184.7 5.1 %collective-permute-start.1 = (bf16[12,12,256]{2,1,0:T(8,128)(2,1)S(1)}, bf16[12,12,256]{2,1,0:T(8,128)(2,1)S(1)}, u32[]{:S(2)}, u32[]{:S(2)}) collective-permute-start(bf16[12,12,256]{2,1,0:T(8,128)(2,1)S(1)} %fusion.421), channel_id=1, source_target_pairs={{64,0},{128,64},{192,128},{256,192},{320,256},{384,320},{448,384},... | collective-permute-start | bytes 221192 | tf_op jit(solution)/shard_map/while/body/eval_jaxpr/ppermute | solution.py:27
  207.3 2.1 fusion.421
  209.4 5.1 %collective-permute-start.1 = (bf16[12,12,256]{2,1,0:T(8,128)(2,1)S(1)}, bf16[12,12,256]{2,1,0:T(8,128)(2,1)S(1)}, u32[]{:S(2)}, u32[]{:S(2)}) collective-permute-start(bf16[12,12,256]{2,1,0:T(8,128)(2,1)S(1)} %fusion.421), channel_id=1, source_target_pairs={{64,0},{128,64},{192,128},{256,192},{320,256},{384,320},{448,384},... | collective-permute-start | bytes 221192 | tf_op jit(solution)/shard_map/while/body/eval_jaxpr/ppermute | solution.py:27
  234.0 5.1 %collective-permute-start.1 = (bf16[12,12,256]{2,1,0:T(8,128)(2,1)S(1)}, bf16[12,12,256]{2,1,0:T(8,128)(2,1)S(1)}, u32[]{:S(2)}, u32[]{:S(2)}) collective-permute-start(bf16[12,12,256]{2,1,0:T(8,128)(2,1)S(1)} %fusion.421), channel_id=1, source_target_pairs={{64,0},{128,64},{192,128},{256,192},{320,256},{384,320},{448,384},... | collective-permute-start | bytes 221192 | tf_op jit(solution)/shard_map/while/body/eval_jaxpr/ppermute | solution.py:27
  256.7 2.1 fusion.421
  258.7 2.2 collective-permute-start.1
  278.4 2.1 fusion.421
  280.5 2.2 collective-permute-start.1
  302.2 2.2 collective-permute-start.1
  321.9 2.1 fusion.421
  324.0 2.2 collective-permute-start.1
  343.7 2.1 fusion.421
  345.8 2.2 collective-permute-start.1
  367.6 2.2 collective-permute-start.1
  384.7 8.0 %collective-permute-start.5 = (bf16[144128]{0:T(1024)(128)(2,1)S(1)}, bf16[144128]{0:T(1024)(128)(2,1)S(1)}, u32[]{:S(2)}, u32[]{:S(2)}) collective-permute-start(bf16[144128]{0:T(1024)(128)(2,1)S(1)} %get-tuple-element.1283), channel_id=1, source_target_pairs={{0,2},{1,3},{2,0},{3,1},{4,6},{5,7},{6,4},{7,5},{8,10},{9,11},{10,... | collective-permute-start | bytes 864776 | tf_op jit(solution)/shard_map/ppermute | solution.py:172
  395.1 5.2 %collective-permute-done.5 = bf16[144128]{0:T(1024)(128)(2,1)S(1)} collective-permute-done((bf16[144128]{0:T(1024)(128)(2,1)S(1)}, bf16[144128]{0:T(1024)(128)(2,1)S(1)}, u32[]{:S(2)}, u32[]{:S(2)}) %collective-permute-start.5) | collective-permute-done | bytes 288288 | tf_op jit(solution)/shard_map/ppermute | solution.py:172
  400.7 5.5 %collective-permute-done.6 = bf16[144128]{0:T(1024)(128)(2,1)S(1)} collective-permute-done((bf16[144128]{0:T(1024)(128)(2,1)S(1)}, bf16[144128]{0:T(1024)(128)(2,1)S(1)}, u32[]{:S(2)}, u32[]{:S(2)}) %collective-permute-start.6) | collective-permute-done | bytes 288288 | tf_op jit(solution)/shard_map/ppermute | solution.py:172
  410.2 4.4 collective-permute-start.7
  414.7 3.3 collective-permute-start.8
  418.0 2.8 collective-permute-start.9
  421.1 2.8 collective-permute-done.8
  424.1 4.0 collective-permute-done.9
  429.4 4.7 %collective-permute-start.10 = (bf16[21248]{0:T(1024)(128)(2,1)S(1)}, bf16[21248]{0:T(1024)(128)(2,1)S(1)}, u32[]{:S(2)}, u32[]{:S(2)}) collective-permute-start(bf16[21248]{0:T(1024)(128)(2,1)S(1)} %get-tuple-element.1285), channel_id=1, source_target_pairs={{0,32},{1,33},{2,34},{3,35},{4,36},{5,37},{6,38},{7,39},{8,40},{9,... | collective-permute-start | bytes 127496 | tf_op jit(solution)/shard_map/ppermute | solution.py:172
  434.1 6.9 %collective-permute-start.11 = (bf16[21248]{0:T(1024)(128)(2,1)S(1)}, bf16[21248]{0:T(1024)(128)(2,1)S(1)}, u32[]{:S(2)}, u32[]{:S(2)}) collective-permute-start(bf16[21248]{0:T(1024)(128)(2,1)S(1)} %get-tuple-element.1286), channel_id=1, source_target_pairs={{0,8},{1,9},{2,10},{3,11},{4,12},{5,13},{6,14},{7,15},{8,0},{9,1},... | collective-permute-start | bytes 127496 | tf_op jit(solution)/shard_map/ppermute | solution.py:172
  441.0 3.0 collective-permute-start.12
  444.5 8.8 %collective-permute-done.12 = bf16[21248]{0:T(1024)(128)(2,1)S(1)} collective-permute-done((bf16[21248]{0:T(1024)(128)(2,1)S(1)}, bf16[21248]{0:T(1024)(128)(2,1)S(1)}, u32[]{:S(2)}, u32[]{:S(2)}) %collective-permute-start.12) | collective-permute-done | bytes 42528 | tf_op jit(solution)/shard_map/ppermute | solution.py:172
  (1067 shorter events, 291.5 us)
Async XLA Ops:
  0.6 8.8 %collective-permute-start.2 = (bf16[6,12,12,256]{3,2,1,0:T(8,128)(2,1)}, bf16[6,12,12,256]{3,2,1,0:T(8,128)(2,1)S(1)}, u32[]{:S(2)}, u32[]{:S(2)}) collective-permute-start(bf16[6,12,12,256]{3,2,1,0:T(8,128)(2,1)} %param.18), channel_id=1, source_target_pairs={{0,1},{1,2},{2,3},{3,4},{4,5},{5,6},{6,7},{7,8},{8,9},{9,10},{10,1... | collective-permute-start | bytes 1327112 | tf_op jit(solution)/shard_map/ppermute | solution.py:16
  2.4 7.0 %collective-permute-start.3 = (bf16[6,12,12,256]{3,2,1,0:T(8,128)(2,1)}, bf16[6,12,12,256]{3,2,1,0:T(8,128)(2,1)S(1)}, u32[]{:S(2)}, u32[]{:S(2)}) collective-permute-start(bf16[6,12,12,256]{3,2,1,0:T(8,128)(2,1)} %param.18), channel_id=1, source_target_pairs={{1,0},{2,1},{3,2},{4,3},{5,4},{6,5},{7,6},{8,7},{9,8},{10,9},{11,1... | collective-permute-start | bytes 1327112 | tf_op jit(solution)/shard_map/ppermute | solution.py:19
  30.6 6.7 %collective-permute-start = (bf16[12,12,256]{2,1,0:T(8,128)(2,1)}, bf16[12,12,256]{2,1,0:T(8,128)(2,1)S(1)}, u32[]{:S(2)}, u32[]{:S(2)}) collective-permute-start(bf16[12,12,256]{2,1,0:T(8,128)(2,1)} %fusion.403), channel_id=1, source_target_pairs={{0,64},{64,128},{128,192},{192,256},{256,320},{320,384},{384,448},... | collective-permute-start | bytes 221192 | tf_op jit(solution)/shard_map/while/body/eval_jaxpr/ppermute | solution.py:27
  46.7 6.7 %collective-permute-start = (bf16[12,12,256]{2,1,0:T(8,128)(2,1)}, bf16[12,12,256]{2,1,0:T(8,128)(2,1)S(1)}, u32[]{:S(2)}, u32[]{:S(2)}) collective-permute-start(bf16[12,12,256]{2,1,0:T(8,128)(2,1)} %fusion.403), channel_id=1, source_target_pairs={{0,64},{64,128},{128,192},{192,256},{256,320},{320,384},{384,448},... | collective-permute-start | bytes 221192 | tf_op jit(solution)/shard_map/while/body/eval_jaxpr/ppermute | solution.py:27
  62.9 6.7 %collective-permute-start = (bf16[12,12,256]{2,1,0:T(8,128)(2,1)}, bf16[12,12,256]{2,1,0:T(8,128)(2,1)S(1)}, u32[]{:S(2)}, u32[]{:S(2)}) collective-permute-start(bf16[12,12,256]{2,1,0:T(8,128)(2,1)} %fusion.403), channel_id=1, source_target_pairs={{0,64},{64,128},{128,192},{192,256},{256,320},{320,384},{384,448},... | collective-permute-start | bytes 221192 | tf_op jit(solution)/shard_map/while/body/eval_jaxpr/ppermute | solution.py:27
  79.1 6.7 %collective-permute-start = (bf16[12,12,256]{2,1,0:T(8,128)(2,1)}, bf16[12,12,256]{2,1,0:T(8,128)(2,1)S(1)}, u32[]{:S(2)}, u32[]{:S(2)}) collective-permute-start(bf16[12,12,256]{2,1,0:T(8,128)(2,1)} %fusion.403), channel_id=1, source_target_pairs={{0,64},{64,128},{128,192},{192,256},{256,320},{320,384},{384,448},... | collective-permute-start | bytes 221192 | tf_op jit(solution)/shard_map/while/body/eval_jaxpr/ppermute | solution.py:27
  95.3 7.1 %collective-permute-start = (bf16[12,12,256]{2,1,0:T(8,128)(2,1)}, bf16[12,12,256]{2,1,0:T(8,128)(2,1)S(1)}, u32[]{:S(2)}, u32[]{:S(2)}) collective-permute-start(bf16[12,12,256]{2,1,0:T(8,128)(2,1)} %fusion.403), channel_id=1, source_target_pairs={{0,64},{64,128},{128,192},{192,256},{256,320},{320,384},{384,448},... | collective-permute-start | bytes 221192 | tf_op jit(solution)/shard_map/while/body/eval_jaxpr/ppermute | solution.py:27
  111.9 7.3 %collective-permute-start = (bf16[12,12,256]{2,1,0:T(8,128)(2,1)}, bf16[12,12,256]{2,1,0:T(8,128)(2,1)S(1)}, u32[]{:S(2)}, u32[]{:S(2)}) collective-permute-start(bf16[12,12,256]{2,1,0:T(8,128)(2,1)} %fusion.403), channel_id=1, source_target_pairs={{0,64},{64,128},{128,192},{192,256},{256,320},{320,384},{384,448},... | collective-permute-start | bytes 221192 | tf_op jit(solution)/shard_map/while/body/eval_jaxpr/ppermute | solution.py:27
  128.6 7.8 %collective-permute-start = (bf16[12,12,256]{2,1,0:T(8,128)(2,1)}, bf16[12,12,256]{2,1,0:T(8,128)(2,1)S(1)}, u32[]{:S(2)}, u32[]{:S(2)}) collective-permute-start(bf16[12,12,256]{2,1,0:T(8,128)(2,1)} %fusion.403), channel_id=1, source_target_pairs={{0,64},{64,128},{128,192},{192,256},{256,320},{320,384},{384,448},... | collective-permute-start | bytes 221192 | tf_op jit(solution)/shard_map/while/body/eval_jaxpr/ppermute | solution.py:27
  145.9 7.9 %collective-permute-start = (bf16[12,12,256]{2,1,0:T(8,128)(2,1)}, bf16[12,12,256]{2,1,0:T(8,128)(2,1)S(1)}, u32[]{:S(2)}, u32[]{:S(2)}) collective-permute-start(bf16[12,12,256]{2,1,0:T(8,128)(2,1)} %fusion.403), channel_id=1, source_target_pairs={{0,64},{64,128},{128,192},{192,256},{256,320},{320,384},{384,448},... | collective-permute-start | bytes 221192 | tf_op jit(solution)/shard_map/while/body/eval_jaxpr/ppermute | solution.py:27
  163.3 7.3 %collective-permute-start = (bf16[12,12,256]{2,1,0:T(8,128)(2,1)}, bf16[12,12,256]{2,1,0:T(8,128)(2,1)S(1)}, u32[]{:S(2)}, u32[]{:S(2)}) collective-permute-start(bf16[12,12,256]{2,1,0:T(8,128)(2,1)} %fusion.403), channel_id=1, source_target_pairs={{0,64},{64,128},{128,192},{192,256},{256,320},{320,384},{384,448},... | collective-permute-start | bytes 221192 | tf_op jit(solution)/shard_map/while/body/eval_jaxpr/ppermute | solution.py:27
  176.0 6.4 %copy-start.3 = (f32[1,256]{1,0:T(1,128)S(1)}, f32[1,256]{1,0:T(1,128)}, u32[]{:S(2)}) copy-start(f32[1,256]{1,0:T(1,128)} %get-tuple-element.1760) | copy-start | bytes 3076 | tf_op jit(solution)/shard_map/while
  176.0 6.4 %copy-start.4 = (f32[1,256]{1,0:T(1,128)S(1)}, f32[1,256]{1,0:T(1,128)}, u32[]{:S(2)}) copy-start(f32[1,256]{1,0:T(1,128)} %get-tuple-element.1761) | copy-start | bytes 3076 | tf_op jit(solution)/shard_map/while
  176.0 6.4 %copy-start.5 = (f32[1,256]{1,0:T(1,128)S(1)}, f32[1,256]{1,0:T(1,128)}, u32[]{:S(2)}) copy-start(f32[1,256]{1,0:T(1,128)} %get-tuple-element.1762) | copy-start | bytes 3076 | tf_op jit(solution)/shard_map/while
  176.0 6.4 %copy-start.6 = (f32[1,256]{1,0:T(1,128)S(1)}, f32[1,256]{1,0:T(1,128)}, u32[]{:S(2)}) copy-start(f32[1,256]{1,0:T(1,128)} %get-tuple-element.1763) | copy-start | bytes 3076 | tf_op jit(solution)/shard_map/while
  176.0 6.4 %copy-start.7 = (f32[1,256]{1,0:T(1,128)S(1)}, f32[1,256]{1,0:T(1,128)}, u32[]{:S(2)}) copy-start(f32[1,256]{1,0:T(1,128)} %get-tuple-element.1764) | copy-start | bytes 3076 | tf_op jit(solution)/shard_map/while
  176.0 6.4 %copy-start.8 = (f32[1,256]{1,0:T(1,128)S(1)}, f32[1,256]{1,0:T(1,128)}, u32[]{:S(2)}) copy-start(f32[1,256]{1,0:T(1,128)} %get-tuple-element.1765) | copy-start | bytes 3076 | tf_op jit(solution)/shard_map/while
  176.1 6.4 %copy-start.9 = (f32[1,256]{1,0:T(1,128)S(1)}, f32[1,256]{1,0:T(1,128)}, u32[]{:S(2)}) copy-start(f32[1,256]{1,0:T(1,128)} %get-tuple-element.1766) | copy-start | bytes 3076 | tf_op jit(solution)/shard_map/while
  176.1 6.4 %copy-start.10 = (f32[1,256]{1,0:T(1,128)S(1)}, f32[1,256]{1,0:T(1,128)}, u32[]{:S(2)}) copy-start(f32[1,256]{1,0:T(1,128)} %get-tuple-element.1767) | copy-start | bytes 3076 | tf_op jit(solution)/shard_map/while
  176.1 6.4 %copy-start.11 = (f32[1,256]{1,0:T(1,128)S(1)}, f32[1,256]{1,0:T(1,128)}, u32[]{:S(2)}) copy-start(f32[1,256]{1,0:T(1,128)} %get-tuple-element.1768) | copy-start | bytes 3076 | tf_op jit(solution)/shard_map/while
  176.1 6.4 %copy-start.12 = (f32[1,256]{1,0:T(1,128)S(1)}, f32[1,256]{1,0:T(1,128)}, u32[]{:S(2)}) copy-start(f32[1,256]{1,0:T(1,128)} %get-tuple-element.1769) | copy-start | bytes 3076 | tf_op jit(solution)/shard_map/while
  176.1 6.4 %copy-start.13 = (f32[1,256]{1,0:T(1,128)S(1)}, f32[1,256]{1,0:T(1,128)}, u32[]{:S(2)}) copy-start(f32[1,256]{1,0:T(1,128)} %get-tuple-element.1770) | copy-start | bytes 3076 | tf_op jit(solution)/shard_map/while
  184.7 10.1 %collective-permute-start.1 = (bf16[12,12,256]{2,1,0:T(8,128)(2,1)S(1)}, bf16[12,12,256]{2,1,0:T(8,128)(2,1)S(1)}, u32[]{:S(2)}, u32[]{:S(2)}) collective-permute-start(bf16[12,12,256]{2,1,0:T(8,128)(2,1)S(1)} %fusion.421), channel_id=1, source_target_pairs={{64,0},{128,64},{192,128},{256,192},{320,256},{384,320},{448,384},... | collective-permute-start | bytes 221192 | tf_op jit(solution)/shard_map/while/body/eval_jaxpr/ppermute | solution.py:27
  200.7 6.4 %copy-start.3 = (f32[1,256]{1,0:T(1,128)S(1)}, f32[1,256]{1,0:T(1,128)}, u32[]{:S(2)}) copy-start(f32[1,256]{1,0:T(1,128)} %get-tuple-element.1760) | copy-start | bytes 3076 | tf_op jit(solution)/shard_map/while
  209.4 10.1 %collective-permute-start.1 = (bf16[12,12,256]{2,1,0:T(8,128)(2,1)S(1)}, bf16[12,12,256]{2,1,0:T(8,128)(2,1)S(1)}, u32[]{:S(2)}, u32[]{:S(2)}) collective-permute-start(bf16[12,12,256]{2,1,0:T(8,128)(2,1)S(1)} %fusion.421), channel_id=1, source_target_pairs={{64,0},{128,64},{192,128},{256,192},{320,256},{384,320},{448,384},... | collective-permute-start | bytes 221192 | tf_op jit(solution)/shard_map/while/body/eval_jaxpr/ppermute | solution.py:27
  225.4 6.4 %copy-start.3 = (f32[1,256]{1,0:T(1,128)S(1)}, f32[1,256]{1,0:T(1,128)}, u32[]{:S(2)}) copy-start(f32[1,256]{1,0:T(1,128)} %get-tuple-element.1760) | copy-start | bytes 3076 | tf_op jit(solution)/shard_map/while
  234.0 10.1 %collective-permute-start.1 = (bf16[12,12,256]{2,1,0:T(8,128)(2,1)S(1)}, bf16[12,12,256]{2,1,0:T(8,128)(2,1)S(1)}, u32[]{:S(2)}, u32[]{:S(2)}) collective-permute-start(bf16[12,12,256]{2,1,0:T(8,128)(2,1)S(1)} %fusion.421), channel_id=1, source_target_pairs={{64,0},{128,64},{192,128},{256,192},{320,256},{384,320},{448,384},... | collective-permute-start | bytes 221192 | tf_op jit(solution)/shard_map/while/body/eval_jaxpr/ppermute | solution.py:27
  250.1 6.4 %copy-start.3 = (f32[1,256]{1,0:T(1,128)S(1)}, f32[1,256]{1,0:T(1,128)}, u32[]{:S(2)}) copy-start(f32[1,256]{1,0:T(1,128)} %get-tuple-element.1760) | copy-start | bytes 3076 | tf_op jit(solution)/shard_map/while
  258.7 7.1 %collective-permute-start.1 = (bf16[12,12,256]{2,1,0:T(8,128)(2,1)S(1)}, bf16[12,12,256]{2,1,0:T(8,128)(2,1)S(1)}, u32[]{:S(2)}, u32[]{:S(2)}) collective-permute-start(bf16[12,12,256]{2,1,0:T(8,128)(2,1)S(1)} %fusion.421), channel_id=1, source_target_pairs={{64,0},{128,64},{192,128},{256,192},{320,256},{384,320},{448,384},... | collective-permute-start | bytes 221192 | tf_op jit(solution)/shard_map/while/body/eval_jaxpr/ppermute | solution.py:27
  271.8 6.4 %copy-start.3 = (f32[1,256]{1,0:T(1,128)S(1)}, f32[1,256]{1,0:T(1,128)}, u32[]{:S(2)}) copy-start(f32[1,256]{1,0:T(1,128)} %get-tuple-element.1760) | copy-start | bytes 3076 | tf_op jit(solution)/shard_map/while
  280.5 7.2 %collective-permute-start.1 = (bf16[12,12,256]{2,1,0:T(8,128)(2,1)S(1)}, bf16[12,12,256]{2,1,0:T(8,128)(2,1)S(1)}, u32[]{:S(2)}, u32[]{:S(2)}) collective-permute-start(bf16[12,12,256]{2,1,0:T(8,128)(2,1)S(1)} %fusion.421), channel_id=1, source_target_pairs={{64,0},{128,64},{192,128},{256,192},{320,256},{384,320},{448,384},... | collective-permute-start | bytes 221192 | tf_op jit(solution)/shard_map/while/body/eval_jaxpr/ppermute | solution.py:27
  293.6 6.4 %copy-start.3 = (f32[1,256]{1,0:T(1,128)S(1)}, f32[1,256]{1,0:T(1,128)}, u32[]{:S(2)}) copy-start(f32[1,256]{1,0:T(1,128)} %get-tuple-element.1760) | copy-start | bytes 3076 | tf_op jit(solution)/shard_map/while
  302.2 7.2 %collective-permute-start.1 = (bf16[12,12,256]{2,1,0:T(8,128)(2,1)S(1)}, bf16[12,12,256]{2,1,0:T(8,128)(2,1)S(1)}, u32[]{:S(2)}, u32[]{:S(2)}) collective-permute-start(bf16[12,12,256]{2,1,0:T(8,128)(2,1)S(1)} %fusion.421), channel_id=1, source_target_pairs={{64,0},{128,64},{192,128},{256,192},{320,256},{384,320},{448,384},... | collective-permute-start | bytes 221192 | tf_op jit(solution)/shard_map/while/body/eval_jaxpr/ppermute | solution.py:27
  315.3 6.4 %copy-start.3 = (f32[1,256]{1,0:T(1,128)S(1)}, f32[1,256]{1,0:T(1,128)}, u32[]{:S(2)}) copy-start(f32[1,256]{1,0:T(1,128)} %get-tuple-element.1760) | copy-start | bytes 3076 | tf_op jit(solution)/shard_map/while
  324.0 7.2 %collective-permute-start.1 = (bf16[12,12,256]{2,1,0:T(8,128)(2,1)S(1)}, bf16[12,12,256]{2,1,0:T(8,128)(2,1)S(1)}, u32[]{:S(2)}, u32[]{:S(2)}) collective-permute-start(bf16[12,12,256]{2,1,0:T(8,128)(2,1)S(1)} %fusion.421), channel_id=1, source_target_pairs={{64,0},{128,64},{192,128},{256,192},{320,256},{384,320},{448,384},... | collective-permute-start | bytes 221192 | tf_op jit(solution)/shard_map/while/body/eval_jaxpr/ppermute | solution.py:27
  337.1 6.4 %copy-start.3 = (f32[1,256]{1,0:T(1,128)S(1)}, f32[1,256]{1,0:T(1,128)}, u32[]{:S(2)}) copy-start(f32[1,256]{1,0:T(1,128)} %get-tuple-element.1760) | copy-start | bytes 3076 | tf_op jit(solution)/shard_map/while
  345.8 7.2 %collective-permute-start.1 = (bf16[12,12,256]{2,1,0:T(8,128)(2,1)S(1)}, bf16[12,12,256]{2,1,0:T(8,128)(2,1)S(1)}, u32[]{:S(2)}, u32[]{:S(2)}) collective-permute-start(bf16[12,12,256]{2,1,0:T(8,128)(2,1)S(1)} %fusion.421), channel_id=1, source_target_pairs={{64,0},{128,64},{192,128},{256,192},{320,256},{384,320},{448,384},... | collective-permute-start | bytes 221192 | tf_op jit(solution)/shard_map/while/body/eval_jaxpr/ppermute | solution.py:27
  358.9 6.4 %copy-start.3 = (f32[1,256]{1,0:T(1,128)S(1)}, f32[1,256]{1,0:T(1,128)}, u32[]{:S(2)}) copy-start(f32[1,256]{1,0:T(1,128)} %get-tuple-element.1760) | copy-start | bytes 3076 | tf_op jit(solution)/shard_map/while
  367.6 7.2 %collective-permute-start.1 = (bf16[12,12,256]{2,1,0:T(8,128)(2,1)S(1)}, bf16[12,12,256]{2,1,0:T(8,128)(2,1)S(1)}, u32[]{:S(2)}, u32[]{:S(2)}) collective-permute-start(bf16[12,12,256]{2,1,0:T(8,128)(2,1)S(1)} %fusion.421), channel_id=1, source_target_pairs={{64,0},{128,64},{192,128},{256,192},{320,256},{384,320},{448,384},... | collective-permute-start | bytes 221192 | tf_op jit(solution)/shard_map/while/body/eval_jaxpr/ppermute | solution.py:27
  382.7 12.0 %collective-permute-start.4 = (bf16[144128]{0:T(1024)(128)(2,1)S(1)}, bf16[144128]{0:T(1024)(128)(2,1)S(1)}, u32[]{:S(2)}, u32[]{:S(2)}) collective-permute-start(bf16[144128]{0:T(1024)(128)(2,1)S(1)} %get-tuple-element.1282), channel_id=1, source_target_pairs={{0,1},{1,0},{2,3},{3,2},{4,5},{5,4},{6,7},{7,6},{8,9},{9,8},{10,11... | collective-permute-start | bytes 864776 | tf_op jit(solution)/shard_map/ppermute | solution.py:172
  384.7 15.7 %collective-permute-start.5 = (bf16[144128]{0:T(1024)(128)(2,1)S(1)}, bf16[144128]{0:T(1024)(128)(2,1)S(1)}, u32[]{:S(2)}, u32[]{:S(2)}) collective-permute-start(bf16[144128]{0:T(1024)(128)(2,1)S(1)} %get-tuple-element.1283), channel_id=1, source_target_pairs={{0,2},{1,3},{2,0},{3,1},{4,6},{5,7},{6,4},{7,5},{8,10},{9,11},{10,... | collective-permute-start | bytes 864776 | tf_op jit(solution)/shard_map/ppermute | solution.py:172
  392.6 13.5 %collective-permute-start.6 = (bf16[144128]{0:T(1024)(128)(2,1)S(1)}, bf16[144128]{0:T(1024)(128)(2,1)S(1)}, u32[]{:S(2)}, u32[]{:S(2)}) collective-permute-start(bf16[144128]{0:T(1024)(128)(2,1)S(1)} %get-tuple-element.1284), channel_id=1, source_target_pairs={{0,3},{1,2},{2,1},{3,0},{4,7},{5,6},{6,5},{7,4},{8,11},{9,10},{10,... | collective-permute-start | bytes 864776 | tf_op jit(solution)/shard_map/ppermute | solution.py:172
  410.2 10.8 %collective-permute-start.7 = (bf16[45824]{0:T(1024)(128)(2,1)S(1)}, bf16[45824]{0:T(1024)(128)(2,1)S(1)}, u32[]{:S(2)}, u32[]{:S(2)}) collective-permute-start(bf16[45824]{0:T(1024)(128)(2,1)S(1)} %get-tuple-element.1288), channel_id=1, source_target_pairs={{0,16},{1,17},{2,18},{3,19},{4,20},{5,21},{6,22},{7,23},{8,24},{9,... | collective-permute-start | bytes 274952 | tf_op jit(solution)/shard_map/ppermute | solution.py:172
  414.7 9.3 %collective-permute-start.8 = (bf16[45824]{0:T(1024)(128)(2,1)S(1)}, bf16[45824]{0:T(1024)(128)(2,1)S(1)}, u32[]{:S(2)}, u32[]{:S(2)}) collective-permute-start(bf16[45824]{0:T(1024)(128)(2,1)S(1)} %get-tuple-element.1289), channel_id=1, source_target_pairs={{0,4},{1,5},{2,6},{3,7},{4,0},{5,1},{6,2},{7,3},{8,12},{9,13},{10,... | collective-permute-start | bytes 274952 | tf_op jit(solution)/shard_map/ppermute | solution.py:172
  418.0 10.0 %collective-permute-start.9 = (bf16[45824]{0:T(1024)(128)(2,1)S(1)}, bf16[45824]{0:T(1024)(128)(2,1)S(1)}, u32[]{:S(2)}, u32[]{:S(2)}) collective-permute-start(bf16[45824]{0:T(1024)(128)(2,1)S(1)} %get-tuple-element.1290), channel_id=1, source_target_pairs={{0,20},{1,21},{2,22},{3,23},{4,16},{5,17},{6,18},{7,19},{8,28},{9,... | collective-permute-start | bytes 274952 | tf_op jit(solution)/shard_map/ppermute | solution.py:172
  429.4 14.7 %collective-permute-start.10 = (bf16[21248]{0:T(1024)(128)(2,1)S(1)}, bf16[21248]{0:T(1024)(128)(2,1)S(1)}, u32[]{:S(2)}, u32[]{:S(2)}) collective-permute-start(bf16[21248]{0:T(1024)(128)(2,1)S(1)} %get-tuple-element.1285), channel_id=1, source_target_pairs={{0,32},{1,33},{2,34},{3,35},{4,36},{5,37},{6,38},{7,39},{8,40},{9,... | collective-permute-start | bytes 127496 | tf_op jit(solution)/shard_map/ppermute | solution.py:172
  434.1 10.3 %collective-permute-start.11 = (bf16[21248]{0:T(1024)(128)(2,1)S(1)}, bf16[21248]{0:T(1024)(128)(2,1)S(1)}, u32[]{:S(2)}, u32[]{:S(2)}) collective-permute-start(bf16[21248]{0:T(1024)(128)(2,1)S(1)} %get-tuple-element.1286), channel_id=1, source_target_pairs={{0,8},{1,9},{2,10},{3,11},{4,12},{5,13},{6,14},{7,15},{8,0},{9,1},... | collective-permute-start | bytes 127496 | tf_op jit(solution)/shard_map/ppermute | solution.py:172
  441.0 12.2 %collective-permute-start.12 = (bf16[21248]{0:T(1024)(128)(2,1)S(1)}, bf16[21248]{0:T(1024)(128)(2,1)S(1)}, u32[]{:S(2)}, u32[]{:S(2)}) collective-permute-start(bf16[21248]{0:T(1024)(128)(2,1)S(1)} %get-tuple-element.1287), channel_id=1, source_target_pairs={{0,40},{1,41},{2,42},{3,43},{4,44},{5,45},{6,46},{7,47},{8,32},{9,... | collective-permute-start | bytes 127496 | tf_op jit(solution)/shard_map/ppermute | solution.py:172
  (244 other events, 1251.5 us)
